TPU v7x, 128 devices: a whole 4x4x4 slice. The times are simulated.
128 devices in a mesh: seq: 16 (over x, y), tensor: 8 (over z, core).
Axes of the slice: x: 4, y: 4, z: 4, core: 2. Of those that a mesh axis runs over, the one named last changes fastest.
Arguments:
- tokens: bfloat16 [12288, 2048], P('seq'), may hold values from -6 to 6
- norm_gain: float32 [2048], replicated, may hold values from 0.1 to 1.9
- query_weight: bfloat16 [2048, 2048], P(None, 'tensor'), may hold values from -0.125 to 0.125
- key_value_matrix: bfloat16 [2048, 4, 128], replicated, may hold values from -0.125 to 0.125
- out_weight: bfloat16 [2048, 2048], replicated, may hold values from -0.125 to 0.125
- cache_pages: bfloat16 [1024, 4, 128, 128], P('seq'), may hold values from -180 to 180, as said below
- page_table: int32 [16, 64], replicated, may hold values from 0 to 1023, as said below
- request_lengths: int32 [80], replicated, may hold values from 1 to 764, as said below
- request_groups: int32 [80], replicated, may hold values from 0 to 15
Outputs:
- projected: bfloat16 [12288, 2048], P('seq', 'tensor')
Inputs may be any that keep to these rules, and one draw needn't show every extreme that they name: `page_table`: every page id appears once. Of the last 16 entries of each row, exactly 1 lie in each block of 64 consecutive ids, the pages held by one seq device. `request_lengths`: the lengths of the 5 requests of one seq device sum to at most 768, and to exactly 768 on at least one device. `cache_pages`: keys in the first 64 entries of the last dimension, values in the rest.
All inputs are finite; a program needn't handle non-finite values.
Results may differ from a plain program's by a relative error of at most 0.012.
The roundings to bfloat16 on the way count: a program that leaves them out, or rounds other values in their place, can miss the bound.
Values may be sent and summed in bfloat16 or wider, within the bound.
No kernel may reach another device: no remote copies, remote signals or barrier semaphores. Data moves between devices by JAX's collectives and lax.ppermute only.
A program may use at most 128 MiB of HBM per device.

v0:
```python
import functools
import math

import jax
import jax.numpy as jnp
from jax import lax
from jax.sharding import PartitionSpec as P
from jax.experimental import pallas as pl
from jax.experimental.pallas import tpu as pltpu

QUERY_HEADS = 32
KEY_VALUE_HEADS = 4
HEAD_SIZE = 64
WINDOW_LENGTH = 2048
DEVICE_REQUESTS = 5
PPG = 64
WP = 16


MASKED_SCORE = -1e30


def normalize(tokens, norm_gain):
    widened = tokens.astype(jnp.float32)
    factor = lax.rsqrt(jnp.mean(widened * widened, axis=-1, keepdims=True) + 1e-05)
    return (widened * factor * norm_gain).astype(jnp.bfloat16)


def layer(
    tokens,
    norm_gain,
    query_weight,
    key_value_matrix,
    out_weight,
    cache_pages,
    page_table,
    request_lengths,
    request_groups,
):
    seq_count = lax.axis_size("seq")
    seq_index = lax.axis_index("seq")
    core_index = lax.axis_index("tc")
    tensor_rank_index = lax.axis_index("tz") * lax.axis_size("tc") + core_index
    row_count = tokens.shape[0]
    resident_heads = query_weight.shape[1] // HEAD_SIZE
    key_value_head = tensor_rank_index * resident_heads // (QUERY_HEADS // KEY_VALUE_HEADS)
    pages_here = cache_pages.shape[0]
    normed = normalize(tokens, norm_gain)
    query_rows = jnp.dot(normed, query_weight, preferred_element_type=jnp.float32).astype(
        jnp.bfloat16
    )
    query_rows = query_rows.reshape(row_count, resident_heads, HEAD_SIZE)
    head_weight = lax.dynamic_index_in_dim(key_value_matrix, key_value_head, 1, keepdims=False)
    new_token_rows = jnp.dot(normed, head_weight, preferred_element_type=jnp.float32).astype(
        jnp.bfloat16
    )
    lengths = lax.dynamic_slice_in_dim(
        request_lengths, seq_index * DEVICE_REQUESTS, DEVICE_REQUESTS
    )
    my_groups = lax.dynamic_slice_in_dim(
        request_groups, seq_index * DEVICE_REQUESTS, DEVICE_REQUESTS
    )
    tail_ids = page_table[:, PPG - WP :]
    holder = tail_ids // pages_here
    local_slot = tail_ids % pages_here
    held_slot = jnp.sum(jnp.where(holder == seq_index, local_slot, 0), axis=1)
    all_groups = request_groups.reshape(seq_count, DEVICE_REQUESTS)
    head_pages = lax.dynamic_index_in_dim(cache_pages, key_value_head, 1, keepdims=False)
    page_part = head_pages.shape[1] // lax.axis_size("tc")
    head_pages = lax.dynamic_slice_in_dim(head_pages, core_index * page_part, page_part, 1)
    outgoing = head_pages[held_slot[all_groups]]
    incoming = lax.all_to_all(outgoing, "seq", 0, 0, tiled=True)
    core_count = lax.axis_size("tc")
    partner = lax.ppermute(incoming, "tc", [(0, 1), (1, 0)])
    source_ids = lax.iota(jnp.int32, seq_count)
    page_order = jnp.sum(
        jnp.where(
            holder[:, :, None] == source_ids[None, None, :],
            lax.iota(jnp.int32, holder.shape[1])[None, :, None],
            0,
        ),
        axis=1,
    )
    page_start = page_order[my_groups][:, :, None] * (page_part * core_count)
    within = lax.iota(jnp.int32, page_part)[None, None, :]
    key_parts = []
    for part, half in ((incoming, core_index), (partner, (core_index + 1) % core_count)):
        positions = (page_start + half * page_part + within).reshape(DEVICE_REQUESTS, 1, -1)
        key_parts.append((part, positions))
    starts = jnp.cumsum(lengths) - lengths
    bounds = jnp.concatenate([starts, starts + lengths]).astype(jnp.int32)
    fresh_pad = new_token_rows
    query_pad = jnp.concatenate(
        [query_rows, jnp.zeros_like(query_rows)], axis=-1
    ).transpose(1, 0, 2)
    attended = attend(bounds, query_pad, key_parts, fresh_pad, WINDOW_LENGTH)
    swap = [(0, 1), (1, 0)]
    z_count = lax.axis_size("tz")
    z_index = lax.axis_index("tz")
    partner_heads = lax.ppermute(attended, "tc", swap)
    first_core = core_index == 0
    chip_heads = jnp.where(
        first_core,
        jnp.concatenate([attended, partner_heads], axis=1),
        jnp.concatenate([partner_heads, attended], axis=1),
    )
    half_rows = row_count // core_count
    my_half = lax.dynamic_slice_in_dim(chip_heads, core_index * half_rows, half_rows, 0)
    sent = jnp.broadcast_to(my_half[None], (z_count,) + my_half.shape)
    chips_heads = lax.all_to_all(sent, "tz", 0, 0, tiled=True)
    chip_width = out_weight.shape[1] // z_count
    chip_columns = lax.dynamic_slice_in_dim(out_weight, z_index * chip_width, chip_width, 1)
    chip_columns = chip_columns.reshape(z_count, my_half.shape[1], chip_width)
    half_out = jnp.einsum(
        "zrj,zjn->rn", chips_heads, chip_columns, preferred_element_type=jnp.float32
    ).astype(jnp.bfloat16)
    columns = chip_width // core_count
    keep = lax.dynamic_slice_in_dim(half_out, core_index * columns, columns, 1)
    give = lax.dynamic_slice_in_dim(half_out, (1 - core_index) * columns, columns, 1)
    got = lax.ppermute(give, "tc", swap)
    projected = jnp.where(
        first_core, jnp.concatenate([keep, got], axis=0), jnp.concatenate([got, keep], axis=0)
    )
    return projected


BLOCK_ROWS = 64


def attend_kernel(window, bounds_ref, q_ref, *refs):
    part_refs = list(zip(refs[0:-2:2], refs[1:-2:2]))
    fresh_ref, o_ref = refs[-2], refs[-1]
    heads, block_rows, _ = q_ref.shape
    stacked = heads * block_rows
    request_count = part_refs[0][0].shape[1]
    row_count = fresh_ref.shape[0]
    first_row = pl.program_id(0) * block_rows
    score_scale = HEAD_SIZE ** (-0.5)
    q = q_ref[...].reshape(stacked, 2 * HEAD_SIZE)
    rows = first_row + lax.broadcasted_iota(jnp.int32, (heads, block_rows, 1), 1).reshape(stacked, 1)
    r_first = jnp.int32(0)
    r_last = jnp.int32(-1)
    for k in range(request_count):
        r_first = r_first + (bounds_ref[request_count + k] <= first_row).astype(jnp.int32)
        r_last = r_last + (bounds_ref[k] < first_row + block_rows).astype(jnp.int32)
    r_last = jnp.minimum(r_last, request_count - 1)
    column = lax.broadcasted_iota(jnp.int32, (stacked, row_count), 1)
    fresh = fresh_ref[...]

    def scores_of(keys):
        return lax.dot_general(
            q, keys, (((1,), (1,)), ((), ())), preferred_element_type=jnp.float32
        ) * score_scale

    def one_request(r, out_acc):
        begin = bounds_ref[r]
        finish = bounds_ref[request_count + r]
        in_request = (rows >= begin) & (rows < finish)
        threshold = jnp.where(in_request, rows - begin + 1, window)
        newest = jnp.where(in_request, rows, -1)
        suffix_mask = (
            (column >= begin) & (column <= newest) & (rows - column < WINDOW_LENGTH)
        )
        pieces = [(fresh, scores_of(fresh), suffix_mask)]
        for keys_ref, positions_ref in part_refs:
            keys = keys_ref[:, r].reshape(-1, 2 * HEAD_SIZE)
            pieces.append((keys, scores_of(keys), positions_ref[r] >= threshold))
        top = jnp.full((stacked, 1), MASKED_SCORE, jnp.float32)
        for _, scores, mask in pieces:
            top = jnp.maximum(
                top, jnp.max(jnp.where(mask, scores, MASKED_SCORE), axis=1, keepdims=True)
            )
        total = jnp.zeros_like(top)
        weighted = jnp.zeros((stacked, 2 * HEAD_SIZE), jnp.float32)
        for keys, scores, mask in pieces:
            raw = jnp.where(mask, jnp.exp(scores - top), 0.0)
            total = total + jnp.sum(raw, axis=1, keepdims=True)
            weighted = weighted + jnp.dot(
                raw.astype(jnp.bfloat16), keys, preferred_element_type=jnp.float32
            )
        safe_total = jnp.where(in_request, total, 1.0)
        return jnp.where(in_request, weighted / safe_total, out_acc)

    out_acc = lax.fori_loop(
        r_first, r_last + 1, one_request, jnp.zeros((stacked, 2 * HEAD_SIZE), jnp.float32)
    )
    result = out_acc[:, HEAD_SIZE:].astype(o_ref.dtype)
    for h in range(heads):
        o_ref[:, h * HEAD_SIZE : (h + 1) * HEAD_SIZE] = result[h * block_rows : (h + 1) * block_rows]


def attend(bounds, query_pad, key_parts, fresh_rows, window):
    heads, row_count, width = query_pad.shape
    block_rows = math.gcd(row_count, BLOCK_ROWS)
    part_specs = []
    part_args = []
    for keys, positions in key_parts:
        part_specs.append(pl.BlockSpec(keys.shape, lambda i, b: (0, 0, 0, 0)))
        part_specs.append(pl.BlockSpec(positions.shape, lambda i, b: (0, 0, 0)))
        part_args.extend([keys, positions])
    return pl.pallas_call(
        functools.partial(attend_kernel, window),
        out_shape=jax.ShapeDtypeStruct((row_count, heads * HEAD_SIZE), jnp.bfloat16),
        grid_spec=pltpu.PrefetchScalarGridSpec(
            num_scalar_prefetch=1,
            grid=(row_count // block_rows,),
            in_specs=[pl.BlockSpec((heads, block_rows, width), lambda i, b: (0, i, 0))]
            + part_specs
            + [pl.BlockSpec((row_count, width), lambda i, b: (0, 0))],
            out_specs=pl.BlockSpec((block_rows, heads * HEAD_SIZE), lambda i, b: (i, 0)),
        ),
        compiler_params=pltpu.CompilerParams(
            dimension_semantics=("arbitrary",), vmem_limit_bytes=48 * 1024 * 1024
        ),
    )(bounds, query_pad, *part_args, fresh_rows)


def solution(mesh):
    cores = 2
    seq_size, tensor_size = mesh.devices.shape
    split_mesh = jax.sharding.Mesh(
        mesh.devices.reshape(seq_size, tensor_size // cores, cores), ("seq", "tz", "tc")
    )
    return jax.shard_map(
        layer,
        mesh=split_mesh,
        in_specs=(
            P("seq", None),
            P(),
            P(None, ("tz", "tc")),
            P(),
            P(),
            P("seq", None, None, None),
            P(),
            P(),
            P(),
        ),
        out_specs=P("seq", ("tz", "tc")),
        check_vma=False,
    )
```

profile of v0, /device:TPU:1, one launch (start us, length us, event | category | flops | bytes accessed | tf_op | source)
XLA Modules:
  0.0 115.2 jit_solution(8442492211631533635)
XLA Ops:
  0.0 0.9 reshape.171
  1.0 0.8 add_select_fusion.1
  1.8 0.9 fusion.10
  2.7 1.2 %gather_fusion = s32[80]{0:T(128)S(1)} fusion(s32[16]{0:T(128)S(1)} %fusion.10, s32[1024]{0:T(1024)S(1)} %pad_clamp_fusion.2), kind=kCustom, calls=%fused_computation | custom fusion | bytes 960 | tf_op jit(solution)/shard_map/gather | solution.py:71
  4.0 0.1 reshape.183
  4.1 1.7 %dynamic-slice_bitcast_fusion = bf16[64,64,128]{2,1,0:T(8,128)(2,1)S(1)} fusion(bf16[64,4,128,128]{3,2,1,0:T(8,128)(2,1)} %param.14, s32[]{:T(128)S(6)} %select_n.103, s32[]{:T(128)S(6)} %select_n.105), kind=kLoop, calls=%fused_computation.12 | loop fusion | bytes 2097160 | tf_op jit(solution)/shard_map/dynamic_slice | solution.py:70
  5.8 1.9 %gather_fusion.1 = bf16[80,64,128]{2,1,0:T(8,128)(2,1)} fusion(bf16[64,64,128]{2,1,0:T(8,128)(2,1)S(1)} %dynamic-slice_bitcast_fusion, s32[1024]{0:T(1024)S(1)} %pad_clamp_fusion.1), kind=kCustom, calls=%fused_computation.1 | custom fusion | bytes 2621760 | tf_op jit(solution)/shard_map/gather | solution.py:71
  7.7 7.7 %all-to-all-start = ((bf16[16,5,64,128]{3,2,1,0:T(8,128)(2,1)}), bf16[16,5,64,128]{3,2,1,0:T(8,128)(2,1)S(1)}, u32[]{:S(2)}, u32[]{:S(2)}) async-start(bf16[16,5,64,128]{3,2,1,0:T(8,128)(2,1)} %bitcast.25), calls=%async_computation | async-start | bytes 2621440 | tf_op jit(solution)/shard_map/all_to_all | solution.py:72
  15.5 0.1 select_reduce_fusion
  15.6 0.6 gather_fusion.2
  16.2 2.7 %fusion = f32[768]{0:T(1024)S(1)} fusion(bf16[768,2048]{1,0:T(8,128)(2,1)} %param.9), kind=kLoop, calls=%fused_computation.5 | loop fusion | flops 4717824 | bytes 3148800 | tf_op jit(solution)/shard_map/reduce_sum | solution.py:25
  19.0 3.3 %convolution_convert_fusion = bf16[768,256]{0,1:T(8,128)(2,1)} fusion(bf16[2048,256]{1,0:T(8,128)(2,1)} %param.11, bf16[768,2048]{1,0:T(8,128)(2,1)S(1)} %copy-done.1, f32[2048]{0:T(1024)S(1)} %copy-done.5, f32[768]{0:T(1024)S(1)} %add_rsqrt_fusion), kind=kOutput, calls=%fused_computation.10 | convolution fusion | flops 811794432 | bytes 4598784 | tf_op jit(solution)/shard_map/dot_general | solution.py:49
  22.3 11.3 %all-to-all-done.refs_0_ = bf16[16,5,64,128]{3,2,1,0:T(8,128)(2,1)S(1)} async-done(((bf16[16,5,64,128]{3,2,1,0:T(8,128)(2,1)}), bf16[16,5,64,128]{3,2,1,0:T(8,128)(2,1)S(1)}, u32[]{:S(2)}, u32[]{:S(2)}) %all-to-all-start) | async-done | bytes 1310752 | tf_op jit(solution)/shard_map/all_to_all | solution.py:72
  33.6 3.5 %collective-permute-start = (bf16[16,5,64,128]{3,2,1,0:T(8,128)(2,1)S(1)}, bf16[16,5,64,128]{3,2,1,0:T(8,128)(2,1)}, u32[]{:S(2)}, u32[]{:S(2)}) collective-permute-start(bf16[16,5,64,128]{3,2,1,0:T(8,128)(2,1)S(1)} %all-to-all-done.refs_0_), channel_id=1, source_target_pairs={{0,1},{1,0},{2,3},{3,2},{4,5},{5,4},{6,7},{7,6},{8,9},{9,8},{10,11... | collective-permute-start | bytes 3932168 | tf_op jit(solution)/shard_map/ppermute | solution.py:74
  37.2 0.2 reduce-window.9
  37.5 0.1 add.189
  37.7 0.1 add.179
  37.8 2.2 %copy.12 = bf16[768,4,64]{2,0,1:T(8,128)(2,1)} copy(bf16[768,4,64]{0,2,1:T(8,128)(2,1)} %bitcast.27) | data formatting | bytes 786432 | tf_op jit(solution)/shard_map/reshape | solution.py:52
  40.1 1.4 %pad_bitcast_fusion.q_ref = bf16[4,768,128]{2,1,0:T(8,128)(2,1)S(1)} fusion(bf16[768,4,64]{2,0,1:T(8,128)(2,1)} %copy.12), kind=kLoop, calls=%fused_computation.17 | loop fusion | bytes 1179648 | tf_op jit(solution)/shard_map/transpose | solution.py:95
  41.6 1.1 constant_dynamic-slice_fusion.3
  42.8 1.1 convolution_convert_fusion.1.refs_4_
  43.9 35.0 %shard_map.91 = bf16[768,256]{1,0:T(8,128)(2,1)} custom-call(s32[10]{0:T(128)S(1)} %pad_add_fusion.bounds_ref, bf16[4,768,128]{2,1,0:T(8,128)(2,1)S(1)} %pad_bitcast_fusion.q_ref, bf16[16,5,64,128]{3,2,1,0:T(8,128)(2,1)S(1)} %all-to-all-done.refs_0_, s32[5,1,1024]{2,1,0:T(1,128)S(1)} %get-tuple-element.10.refs_1_, ...), custom_call_target="tpu_custom_call" | custom-call | tf_op jit(solution)/shard_map/pallas_call | solution.py:201
  78.9 1.9 %collective-permute-done.1 = bf16[768,256]{1,0:T(8,128)(2,1)S(1)} collective-permute-done((bf16[768,256]{1,0:T(8,128)(2,1)}, bf16[768,256]{1,0:T(8,128)(2,1)S(1)}, u32[]{:S(2)}, u32[]{:S(2)}) %collective-permute-start.1) | collective-permute-done | bytes 393248 | tf_op jit(solution)/shard_map/ppermute | solution.py:100
  80.8 1.1 fusion.7
  81.9 1.3 %broadcast_in_dim.21 = bf16[4,384,512]{2,1,0:T(8,128)(2,1)} broadcast(bf16[384,512]{1,0:T(8,128)(2,1)S(1)} %fusion.7), dimensions={1,2} | broadcast | bytes 1966080 | tf_op jit(solution)/shard_map/broadcast_in_dim | solution.py:109
  83.2 5.0 %all-to-all-start.1 = ((bf16[4,384,512]{2,1,0:T(8,128)(2,1)}), bf16[4,384,512]{2,1,0:T(8,128)(2,1)}, u32[]{:S(2)}, u32[]{:S(2)}) async-start(bf16[4,384,512]{2,1,0:T(8,128)(2,1)} %broadcast_in_dim.21), calls=%async_computation.1 | async-start | bytes 3145728 | tf_op jit(solution)/shard_map/all_to_all | solution.py:110
  88.2 3.1 %constant_dynamic-slice_fusion.2 = bf16[2048,512]{1,0:T(8,128)(2,1)} fusion(bf16[2048,2048]{1,0:T(8,128)(2,1)} %param.13, s32[]{:T(128)S(6)} %select_n.116), kind=kLoop, calls=%fused_computation.49 | loop fusion | bytes 4194308 | tf_op jit(solution)/shard_map/dynamic_slice | solution.py:112
  91.3 17.5 %all-to-all-done.1 = bf16[4,384,512]{2,1,0:T(8,128)(2,1)} async-done(((bf16[4,384,512]{2,1,0:T(8,128)(2,1)}), bf16[4,384,512]{2,1,0:T(8,128)(2,1)}, u32[]{:S(2)}, u32[]{:S(2)}) %all-to-all-start.1) | async-done | bytes 1572896 | tf_op jit(solution)/shard_map/all_to_all | solution.py:110
  108.7 3.0 %fusion.3 = bf16[384,512]{1,0:T(8,128)(2,1)S(1)} fusion(bf16[4,384,512]{2,1,0:T(8,128)(2,1)} %all-to-all-done.1, bf16[4,512,512]{2,1,0:T(8,128)(2,1)} %bitcast.26), kind=kOutput, calls=%fused_computation.9 | convolution fusion | flops 805502976 | bytes 4063232 | tf_op jit(solution)/shard_map/zrj,zjn->rn/dot_general | solution.py:114
  111.8 1.4 %collective-permute-start.2 = (bf16[384,256]{1,0:T(8,128)(2,1)S(1)}, bf16[384,256]{1,0:T(8,128)(2,1)S(1)}, u32[]{:S(2)}, u32[]{:S(2)}) collective-permute-start(bf16[384,256]{1,0:T(8,128)(2,1)S(1)} %get-tuple-element.8), channel_id=1, source_target_pairs={{0,1},{1,0},{2,3},{3,2},{4,5},{5,4},{6,7},{7,6},{8,9},{9,8},{10,11... | collective-permute-start | bytes 589832 | tf_op jit(solution)/shard_map/ppermute | solution.py:120
  113.2 1.1 collective-permute-done.2
  114.3 0.9 maximum_select_fusion
  (33 shorter events, 0.9 us)
Async XLA Ops:
  0.0 41.6 %copy-start = (bf16[2048,4,128]{2,1,0:T(4,128)(2,1)S(1)}, bf16[2048,4,128]{2,1,0:T(4,128)(2,1)}, u32[]{:S(2)}) copy-start(bf16[2048,4,128]{2,1,0:T(4,128)(2,1)} %param.12) | copy-start | bytes 6291460
  5.8 9.6 %copy-start.3 = (s32[80]{0:T(128)S(1)}, s32[80]{0:T(128)}, u32[]{:S(2)}) copy-start(s32[80]{0:T(128)} %param.17) | copy-start | bytes 964
  7.7 11.3 %copy-start.5 = (f32[2048]{0:T(1024)S(1)}, f32[2048]{0:T(1024)}, u32[]{:S(2)}) copy-start(f32[2048]{0:T(1024)} %param.10) | copy-start | bytes 24580
  7.7 26.0 %all-to-all-start = ((bf16[16,5,64,128]{3,2,1,0:T(8,128)(2,1)}), bf16[16,5,64,128]{3,2,1,0:T(8,128)(2,1)S(1)}, u32[]{:S(2)}, u32[]{:S(2)}) async-start(bf16[16,5,64,128]{3,2,1,0:T(8,128)(2,1)} %bitcast.25), calls=%async_computation | async-start | bytes 2621440 | tf_op jit(solution)/shard_map/all_to_all | solution.py:72
  16.2 2.8 %copy-start.1 = (bf16[768,2048]{1,0:T(8,128)(2,1)S(1)}, bf16[768,2048]{1,0:T(8,128)(2,1)}, u32[]{:S(2)}) copy-start(bf16[768,2048]{1,0:T(8,128)(2,1)} %param.9) | copy-start | bytes 9437188
  19.0 18.1 %copy-start.4 = (s32[80]{0:T(128)S(1)}, s32[80]{0:T(128)}, u32[]{:S(2)}) copy-start(s32[80]{0:T(128)} %param.16) | copy-start | bytes 964
  33.6 10.2 %collective-permute-start = (bf16[16,5,64,128]{3,2,1,0:T(8,128)(2,1)S(1)}, bf16[16,5,64,128]{3,2,1,0:T(8,128)(2,1)}, u32[]{:S(2)}, u32[]{:S(2)}) collective-permute-start(bf16[16,5,64,128]{3,2,1,0:T(8,128)(2,1)S(1)} %all-to-all-done.refs_0_), channel_id=1, source_target_pairs={{0,1},{1,0},{2,3},{3,2},{4,5},{5,4},{6,7},{7,6},{8,9},{9,8},{10,11... | collective-permute-start | bytes 3932168 | tf_op jit(solution)/shard_map/ppermute | solution.py:74
  40.0 2.8 %copy-start.2 = (bf16[768,2048]{1,0:T(8,128)(2,1)S(1)}, bf16[768,2048]{1,0:T(8,128)(2,1)}, u32[]{:S(2)}) copy-start(bf16[768,2048]{1,0:T(8,128)(2,1)} %param.9) | copy-start | bytes 9437188
  78.9 1.9 %collective-permute-start.1 = (bf16[768,256]{1,0:T(8,128)(2,1)}, bf16[768,256]{1,0:T(8,128)(2,1)S(1)}, u32[]{:S(2)}, u32[]{:S(2)}) collective-permute-start(bf16[768,256]{1,0:T(8,128)(2,1)} %shard_map.91), channel_id=1, source_target_pairs={{0,1},{1,0},{2,3},{3,2},{4,5},{5,4},{6,7},{7,6},{8,9},{9,8},{10,11... | collective-permute-start | bytes 1179656 | tf_op jit(solution)/shard_map/ppermute | solution.py:100
  83.2 25.6 %all-to-all-start.1 = ((bf16[4,384,512]{2,1,0:T(8,128)(2,1)}), bf16[4,384,512]{2,1,0:T(8,128)(2,1)}, u32[]{:S(2)}, u32[]{:S(2)}) async-start(bf16[4,384,512]{2,1,0:T(8,128)(2,1)} %broadcast_in_dim.21), calls=%async_computation.1 | async-start | bytes 3145728 | tf_op jit(solution)/shard_map/all_to_all | solution.py:110
  111.8 2.5 %collective-permute-start.2 = (bf16[384,256]{1,0:T(8,128)(2,1)S(1)}, bf16[384,256]{1,0:T(8,128)(2,1)S(1)}, u32[]{:S(2)}, u32[]{:S(2)}) collective-permute-start(bf16[384,256]{1,0:T(8,128)(2,1)S(1)} %get-tuple-element.8), channel_id=1, source_target_pairs={{0,1},{1,0},{2,3},{3,2},{4,5},{5,4},{6,7},{7,6},{8,9},{9,8},{10,11... | collective-permute-start | bytes 589832 | tf_op jit(solution)/shard_map/ppermute | solution.py:120
where the time goes:
time: 116 us; the launch traced here: 115 us
  Pallas kernels  35 us (30%)
  waiting for transfers between devices  31.8 us (27%)
  starting transfers between devices  17.6 us (15%)
  local copies, waits for them, and re-layouts  16.2 us (14%)
  matrix products  7.44 us (6%)
  other arithmetic  7.02 us (6%)
    pallas_call x1, Pallas kernels, attend(): pl.pallas_call(functools.partial(attend_kernel, window), out_shape=jax.Sh...  35 us
    all_to_all x1, waiting for transfers between devices, layer(): chips_heads = lax.all_to_all(sent, 'tz', 0, 0, tiled=True)  17.5 us
    all_to_all x1, waiting for transfers between devices, layer(): incoming = lax.all_to_all(outgoing, 'seq', 0, 0, tiled=True)  11.3 us
    all_to_all x1, starting transfers between devices, layer(): incoming = lax.all_to_all(outgoing, 'seq', 0, 0, tiled=True)  7.7 us
    all_to_all x1, starting transfers between devices, layer(): chips_heads = lax.all_to_all(sent, 'tz', 0, 0, tiled=True)  5.02 us
    ppermute x1, starting transfers between devices, layer(): partner = lax.ppermute(incoming, 'tc', [(0, 1), (1, 0)])  3.49 us
    dot_general x1, matrix products, layer(): jnp.dot(normed, query_weight, preferred_element_type=jnp.float32)  3.33 us
    gather x3, local copies, waits for them, and re-layouts, layer(): outgoing = head_pages[held_slot[all_groups]]  3.17 us
  transfers between devices with their start and end apart: 5, of which 4 were waited for; matrix products, arithmetic and copies ran while one was open for 14% of the time, Pallas kernels for 0%

commit v1 on v0

--- a/solution.py
+++ b/solution.py
@@ -65,11 +65,12 @@
     local_slot = tail_ids % pages_here
     held_slot = jnp.sum(jnp.where(holder == seq_index, local_slot, 0), axis=1)
     all_groups = request_groups.reshape(seq_count, DEVICE_REQUESTS)
-    head_pages = lax.dynamic_index_in_dim(cache_pages, key_value_head, 1, keepdims=False)
-    page_part = head_pages.shape[1] // lax.axis_size("tc")
-    head_pages = lax.dynamic_slice_in_dim(head_pages, core_index * page_part, page_part, 1)
-    outgoing = head_pages[held_slot[all_groups]]
-    incoming = lax.all_to_all(outgoing, "seq", 0, 0, tiled=True)
+    page_part = cache_pages.shape[2] // lax.axis_size("tc")
+    part_rows = core_index * page_part + lax.iota(jnp.int32, page_part)
+    outgoing = cache_pages[
+        held_slot[all_groups].T[:, :, None], key_value_head, part_rows[None, None, :]
+    ]
+    incoming = lax.all_to_all(outgoing, "seq", 1, 1, tiled=True)
     core_count = lax.axis_size("tc")
     partner = lax.ppermute(incoming, "tc", [(0, 1), (1, 0)])
     source_ids = lax.iota(jnp.int32, seq_count)
@@ -86,7 +87,8 @@
     key_parts = []
     for part, half in ((incoming, core_index), (partner, (core_index + 1) % core_count)):
         positions = (page_start + half * page_part + within).reshape(DEVICE_REQUESTS, 1, -1)
-        key_parts.append((part, positions))
+        keys = part.reshape(DEVICE_REQUESTS, -1, 2 * HEAD_SIZE)
+        key_parts.append((keys, positions))
     starts = jnp.cumsum(lengths) - lengths
     bounds = jnp.concatenate([starts, starts + lengths]).astype(jnp.int32)
     fresh_pad = new_token_rows
@@ -132,7 +134,7 @@
     fresh_ref, o_ref = refs[-2], refs[-1]
     heads, block_rows, _ = q_ref.shape
     stacked = heads * block_rows
-    request_count = part_refs[0][0].shape[1]
+    request_count = part_refs[0][0].shape[0]
     row_count = fresh_ref.shape[0]
     first_row = pl.program_id(0) * block_rows
     score_scale = HEAD_SIZE ** (-0.5)
@@ -163,7 +165,7 @@
         )
         pieces = [(fresh, scores_of(fresh), suffix_mask)]
         for keys_ref, positions_ref in part_refs:
-            keys = keys_ref[:, r].reshape(-1, 2 * HEAD_SIZE)
+            keys = keys_ref[r]
             pieces.append((keys, scores_of(keys), positions_ref[r] >= threshold))
         top = jnp.full((stacked, 1), MASKED_SCORE, jnp.float32)
         for _, scores, mask in pieces:
@@ -195,7 +197,7 @@
     part_specs = []
     part_args = []
     for keys, positions in key_parts:
-        part_specs.append(pl.BlockSpec(keys.shape, lambda i, b: (0, 0, 0, 0)))
+        part_specs.append(pl.BlockSpec(keys.shape, lambda i, b: (0, 0, 0)))
         part_specs.append(pl.BlockSpec(positions.shape, lambda i, b: (0, 0, 0)))
         part_args.extend([keys, positions])
     return pl.pallas_call(

time: 116 us -> 182 us (1.57)
  local copies, waits for them, and re-layouts: 16.2 us -> 84.9 us
    gather x3 -> x4, local copies, waits for them, and re-layouts: 3.17 us -> 72.1 us  [the longest x2 70.8 us: layer(): cache_pages[held_slot[all_groups].T[:, :, None], key_value_head, part_row...]
  transfers between devices with their start and end apart: 5 -> 5, of which waited for: 4 -> 4; matrix products, arithmetic and copies ran while one was open for 14% -> 9% of each run, Pallas kernels for 0% -> 0%
where the time goes in v1:
time: 182 us; the launch traced here: 181 us
  local copies, waits for them, and re-layouts  84.9 us (47%)
  Pallas kernels  33.3 us (18%)
  waiting for transfers between devices  31.1 us (17%)
  starting transfers between devices  17.7 us (10%)
  matrix products  7.42 us (4%)
  other arithmetic  6.21 us (3%)
    gather x2, local copies, waits for them, and re-layouts, layer(): cache_pages[held_slot[all_groups].T[:, :, None], key_value_head, part_row...  70.8 us
    pallas_call x1, Pallas kernels, attend(): pl.pallas_call(functools.partial(attend_kernel, window), out_shape=jax.Sh...  33.3 us
    all_to_all x1, waiting for transfers between devices, layer(): chips_heads = lax.all_to_all(sent, 'tz', 0, 0, tiled=True)  17.5 us
    all_to_all x1, waiting for transfers between devices, layer(): incoming = lax.all_to_all(outgoing, 'seq', 1, 1, tiled=True)  10.8 us
    all_to_all x1, starting transfers between devices, layer(): incoming = lax.all_to_all(outgoing, 'seq', 1, 1, tiled=True)  7.7 us
    all_to_all x1, starting transfers between devices, layer(): chips_heads = lax.all_to_all(sent, 'tz', 0, 0, tiled=True)  5.02 us
  transfers between devices with their start and end apart: 5, of which 4 were waited for; matrix products, arithmetic and copies ran while one was open for 9% of the time, Pallas kernels for 0%

profile of v1, /device:TPU:1, one launch (start us, length us, event | category | flops | bytes accessed | tf_op | source)
XLA Modules:
  0.0 180.9 jit_solution(7785031171133887578)
XLA Ops:
  0.0 0.9 add_select_fusion.1
  0.9 0.7 reshape.176
  1.8 0.9 fusion.10
  2.7 1.2 gather_fusion
  4.3 69.6 %gather_fusion.1 = bf16[5120,128]{1,0:T(8,128)(2,1)S(1)} fusion(bf16[64,4,128,128]{3,2,1,0:T(8,128)(2,1)} %param.14, s32[5120]{0:T(1024)S(1)} %reshape.188), kind=kCustom, calls=%fused_computation.1 | custom fusion | bytes 2682880 | tf_op jit(solution)/shard_map/gather | solution.py:70
  73.9 1.2 copy.22
  75.1 7.7 %all-to-all-start = ((bf16[5,16,64,128]{3,2,0,1:T(8,128)(2,1)}), bf16[5,16,64,128]{3,2,0,1:T(8,128)(2,1)S(1)}, u32[]{:S(2)}, u32[]{:S(2)}) async-start(bf16[5,16,64,128]{3,2,0,1:T(8,128)(2,1)} %copy.22), calls=%async_computation | async-start | bytes 2621440 | tf_op jit(solution)/shard_map/all_to_all | solution.py:73
  82.9 0.1 select_reduce_fusion
  83.0 0.6 gather_fusion.2
  83.7 0.1 add.187
  83.8 0.1 add.197
  84.0 2.7 %fusion = f32[768]{0:T(1024)S(1)} fusion(bf16[768,2048]{1,0:T(8,128)(2,1)} %param.9), kind=kLoop, calls=%fused_computation.5 | loop fusion | flops 4717824 | bytes 3148800 | tf_op jit(solution)/shard_map/reduce_sum | solution.py:25
  86.9 3.3 %convolution_convert_fusion = bf16[768,256]{0,1:T(8,128)(2,1)} fusion(bf16[2048,256]{1,0:T(8,128)(2,1)} %param.11, bf16[768,2048]{1,0:T(8,128)(2,1)S(1)} %copy-done.1, f32[2048]{0:T(1024)S(1)} %copy-done.5, f32[768]{0:T(1024)S(1)} %add_rsqrt_fusion), kind=kOutput, calls=%fused_computation.10 | convolution fusion | flops 811794432 | bytes 4598784 | tf_op jit(solution)/shard_map/dot_general | solution.py:49
  90.2 10.8 %all-to-all-done = bf16[5,16,64,128]{3,2,0,1:T(8,128)(2,1)S(1)} async-done(((bf16[5,16,64,128]{3,2,0,1:T(8,128)(2,1)}), bf16[5,16,64,128]{3,2,0,1:T(8,128)(2,1)S(1)}, u32[]{:S(2)}, u32[]{:S(2)}) %all-to-all-start) | async-done | bytes 1310752 | tf_op jit(solution)/shard_map/all_to_all | solution.py:73
  101.0 3.5 %collective-permute-start = (bf16[5,16,64,128]{3,2,0,1:T(8,128)(2,1)S(1)}, bf16[5,16,64,128]{3,2,0,1:T(8,128)(2,1)}, u32[]{:S(2)}, u32[]{:S(2)}) collective-permute-start(bf16[5,16,64,128]{3,2,0,1:T(8,128)(2,1)S(1)} %all-to-all-done), channel_id=1, source_target_pairs={{0,1},{1,0},{2,3},{3,2},{4,5},{5,4},{6,7},{7,6},{8,9},{9,8},{10,11... | collective-permute-start | bytes 3932168 | tf_op jit(solution)/shard_map/ppermute | solution.py:75
  104.6 0.2 reduce-window.9
  104.8 2.2 %copy.20 = bf16[768,4,64]{2,0,1:T(8,128)(2,1)} copy(bf16[768,4,64]{0,2,1:T(8,128)(2,1)} %bitcast.33) | data formatting | bytes 786432 | tf_op jit(solution)/shard_map/reshape | solution.py:52
  107.1 1.4 pad_bitcast_fusion.q_ref
  108.6 1.1 constant_dynamic-slice_fusion.3
  109.8 1.0 convolution_convert_fusion.1.refs_4_
  110.8 0.1 copy.23
  111.0 1.4 copy.24
  112.4 33.3 %shard_map.91 = bf16[768,256]{1,0:T(8,128)(2,1)S(1)} custom-call(s32[10]{0:T(128)S(1)} %pad_add_fusion.bounds_ref, bf16[4,768,128]{2,1,0:T(8,128)(2,1)S(1)} %pad_bitcast_fusion.q_ref, bf16[5,1024,128]{2,1,0:T(8,128)(2,1)S(1)} %bitcast.29, s32[5,1,1024]{2,1,0:T(1,128)S(1)} %get-tuple-element.10.refs_1_, bf16[5,1024,128]{2,1,0:T(8,128)(2,1)S(1)} %bitcast.30, ...), custom_call_target="tpu_custom_call" | custom-call | tf_op jit(solution)/shard_map/pallas_call | solution.py:203
  145.8 1.7 collective-permute-done.1
  147.6 1.3 broadcast_in_dim.30
  148.9 5.0 %all-to-all-start.1 = ((bf16[4,384,512]{2,1,0:T(8,128)(2,1)}), bf16[4,384,512]{2,1,0:T(8,128)(2,1)}, u32[]{:S(2)}, u32[]{:S(2)}) async-start(bf16[4,384,512]{2,1,0:T(8,128)(2,1)} %broadcast_in_dim.30), calls=%async_computation.1 | async-start | bytes 3145728 | tf_op jit(solution)/shard_map/all_to_all | solution.py:112
  153.9 3.1 %constant_dynamic-slice_fusion.2 = bf16[2048,512]{1,0:T(8,128)(2,1)} fusion(bf16[2048,2048]{1,0:T(8,128)(2,1)} %param.13, s32[]{:T(128)S(6)} %select_n.107), kind=kLoop, calls=%fused_computation.52 | loop fusion | bytes 4194308 | tf_op jit(solution)/shard_map/dynamic_slice | solution.py:114
  157.0 17.5 %all-to-all-done.1 = bf16[4,384,512]{2,1,0:T(8,128)(2,1)} async-done(((bf16[4,384,512]{2,1,0:T(8,128)(2,1)}), bf16[4,384,512]{2,1,0:T(8,128)(2,1)}, u32[]{:S(2)}, u32[]{:S(2)}) %all-to-all-start.1) | async-done | bytes 1572896 | tf_op jit(solution)/shard_map/all_to_all | solution.py:112
  174.4 3.0 %fusion.3 = bf16[384,512]{1,0:T(8,128)(2,1)S(1)} fusion(bf16[4,384,512]{2,1,0:T(8,128)(2,1)} %all-to-all-done.1, bf16[4,512,512]{2,1,0:T(8,128)(2,1)} %bitcast.32), kind=kOutput, calls=%fused_computation.9 | convolution fusion | flops 805502976 | bytes 4063232 | tf_op jit(solution)/shard_map/zrj,zjn->rn/dot_general | solution.py:116
  177.5 1.4 collective-permute-start.2
  178.9 1.1 collective-permute-done.2
  180.0 0.9 maximum_select_fusion
  (37 shorter events, 1.3 us)
Async XLA Ops:
  0.0 108.6 %copy-start = (bf16[2048,4,128]{2,1,0:T(4,128)(2,1)S(1)}, bf16[2048,4,128]{2,1,0:T(4,128)(2,1)}, u32[]{:S(2)}) copy-start(bf16[2048,4,128]{2,1,0:T(4,128)(2,1)} %param.12) | copy-start | bytes 6291460
  73.9 8.9 %copy-start.3 = (s32[80]{0:T(128)S(1)}, s32[80]{0:T(128)}, u32[]{:S(2)}) copy-start(s32[80]{0:T(128)} %param.17) | copy-start | bytes 964
  75.1 11.7 %copy-start.5 = (f32[2048]{0:T(1024)S(1)}, f32[2048]{0:T(1024)}, u32[]{:S(2)}) copy-start(f32[2048]{0:T(1024)} %param.10) | copy-start | bytes 24580
  75.1 26.0 %all-to-all-start = ((bf16[5,16,64,128]{3,2,0,1:T(8,128)(2,1)}), bf16[5,16,64,128]{3,2,0,1:T(8,128)(2,1)S(1)}, u32[]{:S(2)}, u32[]{:S(2)}) async-start(bf16[5,16,64,128]{3,2,0,1:T(8,128)(2,1)} %copy.22), calls=%async_computation | async-start | bytes 2621440 | tf_op jit(solution)/shard_map/all_to_all | solution.py:73
  84.0 2.8 %copy-start.1 = (bf16[768,2048]{1,0:T(8,128)(2,1)S(1)}, bf16[768,2048]{1,0:T(8,128)(2,1)}, u32[]{:S(2)}) copy-start(bf16[768,2048]{1,0:T(8,128)(2,1)} %param.9) | copy-start | bytes 9437188
  86.9 17.7 %copy-start.4 = (s32[80]{0:T(128)S(1)}, s32[80]{0:T(128)}, u32[]{:S(2)}) copy-start(s32[80]{0:T(128)} %param.16) | copy-start | bytes 964
  101.0 9.9 %collective-permute-start = (bf16[5,16,64,128]{3,2,0,1:T(8,128)(2,1)S(1)}, bf16[5,16,64,128]{3,2,0,1:T(8,128)(2,1)}, u32[]{:S(2)}, u32[]{:S(2)}) collective-permute-start(bf16[5,16,64,128]{3,2,0,1:T(8,128)(2,1)S(1)} %all-to-all-done), channel_id=1, source_target_pairs={{0,1},{1,0},{2,3},{3,2},{4,5},{5,4},{6,7},{7,6},{8,9},{9,8},{10,11... | collective-permute-start | bytes 3932168 | tf_op jit(solution)/shard_map/ppermute | solution.py:75
  107.0 2.8 %copy-start.2 = (bf16[768,2048]{1,0:T(8,128)(2,1)S(1)}, bf16[768,2048]{1,0:T(8,128)(2,1)}, u32[]{:S(2)}) copy-start(bf16[768,2048]{1,0:T(8,128)(2,1)} %param.9) | copy-start | bytes 9437188
  145.7 1.8 collective-permute-start.1
  148.9 25.6 %all-to-all-start.1 = ((bf16[4,384,512]{2,1,0:T(8,128)(2,1)}), bf16[4,384,512]{2,1,0:T(8,128)(2,1)}, u32[]{:S(2)}, u32[]{:S(2)}) async-start(bf16[4,384,512]{2,1,0:T(8,128)(2,1)} %broadcast_in_dim.30), calls=%async_computation.1 | async-start | bytes 3145728 | tf_op jit(solution)/shard_map/all_to_all | solution.py:112
  177.5 2.5 %collective-permute-start.2 = (bf16[384,256]{1,0:T(8,128)(2,1)S(1)}, bf16[384,256]{1,0:T(8,128)(2,1)S(1)}, u32[]{:S(2)}, u32[]{:S(2)}) collective-permute-start(bf16[384,256]{1,0:T(8,128)(2,1)S(1)} %get-tuple-element.8), channel_id=1, source_target_pairs={{0,1},{1,0},{2,3},{3,2},{4,5},{5,4},{6,7},{7,6},{8,9},{9,8},{10,11... | collective-permute-start | bytes 589832 | tf_op jit(solution)/shard_map/ppermute | solution.py:122

commit v2 on v1

--- a/solution.py
+++ b/solution.py
@@ -65,11 +65,10 @@
     local_slot = tail_ids % pages_here
     held_slot = jnp.sum(jnp.where(holder == seq_index, local_slot, 0), axis=1)
     all_groups = request_groups.reshape(seq_count, DEVICE_REQUESTS)
-    page_part = cache_pages.shape[2] // lax.axis_size("tc")
-    part_rows = core_index * page_part + lax.iota(jnp.int32, page_part)
-    outgoing = cache_pages[
-        held_slot[all_groups].T[:, :, None], key_value_head, part_rows[None, None, :]
-    ]
+    head_pages = lax.dynamic_index_in_dim(cache_pages, key_value_head, 1, keepdims=False)
+    page_part = head_pages.shape[1] // lax.axis_size("tc")
+    head_pages = lax.dynamic_slice_in_dim(head_pages, core_index * page_part, page_part, 1)
+    outgoing = head_pages[held_slot[all_groups].T]
     incoming = lax.all_to_all(outgoing, "seq", 1, 1, tiled=True)
     core_count = lax.axis_size("tc")
     partner = lax.ppermute(incoming, "tc", [(0, 1), (1, 0)])
@@ -126,7 +125,7 @@
     return projected
 
 
-BLOCK_ROWS = 64
+BLOCK_ROWS = 128
 
 
 def attend_kernel(window, bounds_ref, q_ref, *refs):

time: 182 us -> 132 us (0.73)
  local copies, waits for them, and re-layouts: 84.9 us -> 20.1 us
  Pallas kernels: 33.3 us -> 48.7 us
    gather x4, local copies, waits for them, and re-layouts: 72.1 us -> 5.66 us  [layer(): outgoing = head_pages[held_slot[all_groups].T]]
    pallas_call x1, Pallas kernels: 33.3 us -> 48.7 us  [attend(): pl.pallas_call(functools.partial(attend_kernel, window), out_shape=jax.Sh...]
  transfers between devices with their start and end apart: 5 -> 5, of which waited for: 4 -> 4; matrix products, arithmetic and copies ran while one was open for 9% -> 13% of each run, Pallas kernels for 0% -> 0%
where the time goes in v2:
time: 132 us; the launch traced here: 131 us
  Pallas kernels  48.7 us (37%)
  waiting for transfers between devices  31.1 us (24%)
  local copies, waits for them, and re-layouts  20.1 us (15%)
  starting transfers between devices  17.7 us (13%)
  matrix products  7.42 us (6%)
  other arithmetic  6.13 us (5%)
    pallas_call x1, Pallas kernels, attend(): pl.pallas_call(functools.partial(attend_kernel, window), out_shape=jax.Sh...  48.7 us
    all_to_all x1, waiting for transfers between devices, layer(): chips_heads = lax.all_to_all(sent, 'tz', 0, 0, tiled=True)  17.5 us
    all_to_all x1, waiting for transfers between devices, layer(): incoming = lax.all_to_all(outgoing, 'seq', 1, 1, tiled=True)  10.8 us
    all_to_all x1, starting transfers between devices, layer(): incoming = lax.all_to_all(outgoing, 'seq', 1, 1, tiled=True)  7.7 us
    gather x4, local copies, waits for them, and re-layouts, layer(): outgoing = head_pages[held_slot[all_groups].T]  5.66 us
    all_to_all x1, starting transfers between devices, layer(): chips_heads = lax.all_to_all(sent, 'tz', 0, 0, tiled=True)  5.02 us
    ppermute x1, starting transfers between devices, layer(): partner = lax.ppermute(incoming, 'tc', [(0, 1), (1, 0)])  3.49 us
    dot_general x1, matrix products, layer(): jnp.dot(normed, query_weight, preferred_element_type=jnp.float32)  3.33 us
  transfers between devices with their start and end apart: 5, of which 4 were waited for; matrix products, arithmetic and copies ran while one was open for 13% of the time, Pallas kernels for 0%

profile of v2, /device:TPU:1, one launch (start us, length us, event | category | flops | bytes accessed | tf_op | source)
XLA Modules:
  0.0 131.4 jit_solution(16964998927053564702)
XLA Ops:
  0.0 0.9 add_select_fusion.1
  0.9 0.7 reshape.164
  1.8 0.9 fusion.10
  2.7 1.2 gather_fusion
  4.2 1.7 %dynamic-slice_bitcast_fusion = bf16[64,64,128]{2,1,0:T(8,128)(2,1)S(1)} fusion(bf16[64,4,128,128]{3,2,1,0:T(8,128)(2,1)} %param.14, s32[]{:T(128)S(6)} %select_n.96, s32[]{:T(128)S(6)} %select_n.98), kind=kLoop, calls=%fused_computation.12 | loop fusion | bytes 2097160 | tf_op jit(solution)/shard_map/dynamic_slice | solution.py:70
  5.9 1.9 %gather_fusion.1 = bf16[80,64,128]{2,1,0:T(8,128)(2,1)} fusion(bf16[64,64,128]{2,1,0:T(8,128)(2,1)S(1)} %dynamic-slice_bitcast_fusion, s32[1024]{0:T(1024)S(1)} %pad_clamp_fusion.1), kind=kCustom, calls=%fused_computation.1 | custom fusion | bytes 2621760 | tf_op jit(solution)/shard_map/gather | solution.py:71
  7.7 2.5 %copy.27 = bf16[5,16,64,128]{3,2,0,1:T(8,128)(2,1)} copy(bf16[5,16,64,128]{3,2,1,0:T(8,128)(2,1)} %bitcast.29) | data formatting | bytes 2621440 | tf_op jit(solution)/shard_map/gather | solution.py:71
  10.2 7.7 %all-to-all-start = ((bf16[5,16,64,128]{3,2,0,1:T(8,128)(2,1)}), bf16[5,16,64,128]{3,2,0,1:T(8,128)(2,1)S(1)}, u32[]{:S(2)}, u32[]{:S(2)}) async-start(bf16[5,16,64,128]{3,2,0,1:T(8,128)(2,1)} %copy.27), calls=%async_computation | async-start | bytes 2621440 | tf_op jit(solution)/shard_map/all_to_all | solution.py:72
  18.0 0.1 select_reduce_fusion
  18.2 0.6 gather_fusion.2
  18.8 0.1 add.172
  19.2 2.7 %fusion = f32[768]{0:T(1024)S(1)} fusion(bf16[768,2048]{1,0:T(8,128)(2,1)} %param.9), kind=kLoop, calls=%fused_computation.5 | loop fusion | flops 4717824 | bytes 3148800 | tf_op jit(solution)/shard_map/reduce_sum | solution.py:25
  22.0 3.3 %convolution_convert_fusion = bf16[768,256]{0,1:T(8,128)(2,1)} fusion(bf16[2048,256]{1,0:T(8,128)(2,1)} %param.11, bf16[768,2048]{1,0:T(8,128)(2,1)S(1)} %copy-done.1, f32[2048]{0:T(1024)S(1)} %copy-done.5, f32[768]{0:T(1024)S(1)} %add_rsqrt_fusion), kind=kOutput, calls=%fused_computation.10 | convolution fusion | flops 811794432 | bytes 4598784 | tf_op jit(solution)/shard_map/dot_general | solution.py:49
  25.3 10.8 %all-to-all-done = bf16[5,16,64,128]{3,2,0,1:T(8,128)(2,1)S(1)} async-done(((bf16[5,16,64,128]{3,2,0,1:T(8,128)(2,1)}), bf16[5,16,64,128]{3,2,0,1:T(8,128)(2,1)S(1)}, u32[]{:S(2)}, u32[]{:S(2)}) %all-to-all-start) | async-done | bytes 1310752 | tf_op jit(solution)/shard_map/all_to_all | solution.py:72
  36.2 3.5 %collective-permute-start = (bf16[5,16,64,128]{3,2,0,1:T(8,128)(2,1)S(1)}, bf16[5,16,64,128]{3,2,0,1:T(8,128)(2,1)}, u32[]{:S(2)}, u32[]{:S(2)}) collective-permute-start(bf16[5,16,64,128]{3,2,0,1:T(8,128)(2,1)S(1)} %all-to-all-done), channel_id=1, source_target_pairs={{0,1},{1,0},{2,3},{3,2},{4,5},{5,4},{6,7},{7,6},{8,9},{9,8},{10,11... | collective-permute-start | bytes 3932168 | tf_op jit(solution)/shard_map/ppermute | solution.py:74
  39.8 0.2 reduce-window.9
  39.9 2.2 %copy.25 = bf16[768,4,64]{2,0,1:T(8,128)(2,1)} copy(bf16[768,4,64]{0,2,1:T(8,128)(2,1)} %bitcast.31) | data formatting | bytes 786432 | tf_op jit(solution)/shard_map/reshape | solution.py:52
  42.3 1.4 %pad_bitcast_fusion.q_ref = bf16[4,768,128]{2,1,0:T(8,128)(2,1)S(1)} fusion(bf16[768,4,64]{2,0,1:T(8,128)(2,1)} %copy.25), kind=kLoop, calls=%fused_computation.17 | loop fusion | bytes 1179648 | tf_op jit(solution)/shard_map/transpose | solution.py:96
  43.7 1.1 constant_dynamic-slice_fusion.3
  44.9 1.0 convolution_convert_fusion.1.refs_4_
  46.0 0.1 copy.28
  46.1 1.4 %copy.29 = bf16[5,16,64,128]{3,2,1,0:T(8,128)(2,1)S(1)} copy(bf16[5,16,64,128]{3,2,0,1:T(8,128)(2,1)} %collective-permute-done) | data formatting | bytes 2621440 | tf_op jit(solution)/shard_map/ppermute | solution.py:74
  47.5 48.7 %shard_map.91 = bf16[768,256]{1,0:T(8,128)(2,1)S(1)} custom-call(s32[10]{0:T(128)S(1)} %pad_add_fusion.bounds_ref, bf16[4,768,128]{2,1,0:T(8,128)(2,1)S(1)} %pad_bitcast_fusion.q_ref, bf16[5,1024,128]{2,1,0:T(8,128)(2,1)S(1)} %bitcast.27, s32[5,1,1024]{2,1,0:T(1,128)S(1)} %get-tuple-element.10.refs_1_, bf16[5,1024,128]{2,1,0:T(8,128)(2,1)S(1)} %bitcast.28, ...), custom_call_target="tpu_custom_call" | custom-call | tf_op jit(solution)/shard_map/pallas_call | solution.py:202
  96.3 1.7 %collective-permute-done.1 = bf16[768,256]{1,0:T(8,128)(2,1)S(1)} collective-permute-done((bf16[768,256]{1,0:T(8,128)(2,1)S(1)}, bf16[768,256]{1,0:T(8,128)(2,1)S(1)}, u32[]{:S(2)}, u32[]{:S(2)}) %collective-permute-start.1) | collective-permute-done | bytes 393248 | tf_op jit(solution)/shard_map/ppermute | solution.py:101
  98.1 1.3 broadcast_in_dim.24
  99.4 5.0 %all-to-all-start.1 = ((bf16[4,384,512]{2,1,0:T(8,128)(2,1)}), bf16[4,384,512]{2,1,0:T(8,128)(2,1)}, u32[]{:S(2)}, u32[]{:S(2)}) async-start(bf16[4,384,512]{2,1,0:T(8,128)(2,1)} %broadcast_in_dim.24), calls=%async_computation.1 | async-start | bytes 3145728 | tf_op jit(solution)/shard_map/all_to_all | solution.py:111
  104.4 3.1 %constant_dynamic-slice_fusion.2 = bf16[2048,512]{1,0:T(8,128)(2,1)} fusion(bf16[2048,2048]{1,0:T(8,128)(2,1)} %param.13, s32[]{:T(128)S(6)} %select_n.109), kind=kLoop, calls=%fused_computation.49 | loop fusion | bytes 4194308 | tf_op jit(solution)/shard_map/dynamic_slice | solution.py:113
  107.5 17.5 %all-to-all-done.1 = bf16[4,384,512]{2,1,0:T(8,128)(2,1)} async-done(((bf16[4,384,512]{2,1,0:T(8,128)(2,1)}), bf16[4,384,512]{2,1,0:T(8,128)(2,1)}, u32[]{:S(2)}, u32[]{:S(2)}) %all-to-all-start.1) | async-done | bytes 1572896 | tf_op jit(solution)/shard_map/all_to_all | solution.py:111
  124.9 3.0 %fusion.3 = bf16[384,512]{1,0:T(8,128)(2,1)S(1)} fusion(bf16[4,384,512]{2,1,0:T(8,128)(2,1)} %all-to-all-done.1, bf16[4,512,512]{2,1,0:T(8,128)(2,1)} %bitcast.30), kind=kOutput, calls=%fused_computation.9 | convolution fusion | flops 805502976 | bytes 4063232 | tf_op jit(solution)/shard_map/zrj,zjn->rn/dot_general | solution.py:115
  128.0 1.4 %collective-permute-start.2 = (bf16[384,256]{1,0:T(8,128)(2,1)S(1)}, bf16[384,256]{1,0:T(8,128)(2,1)S(1)}, u32[]{:S(2)}, u32[]{:S(2)}) collective-permute-start(bf16[384,256]{1,0:T(8,128)(2,1)S(1)} %get-tuple-element.8), channel_id=1, source_target_pairs={{0,1},{1,0},{2,3},{3,2},{4,5},{5,4},{6,7},{7,6},{8,9},{9,8},{10,11... | collective-permute-start | bytes 589832 | tf_op jit(solution)/shard_map/ppermute | solution.py:121
  129.4 1.1 collective-permute-done.2
  130.5 0.9 maximum_select_fusion
  (37 shorter events, 1.4 us)
Async XLA Ops:
  0.0 43.7 %copy-start = (bf16[2048,4,128]{2,1,0:T(4,128)(2,1)S(1)}, bf16[2048,4,128]{2,1,0:T(4,128)(2,1)}, u32[]{:S(2)}) copy-start(bf16[2048,4,128]{2,1,0:T(4,128)(2,1)} %param.12) | copy-start | bytes 6291460
  7.7 10.2 %copy-start.3 = (s32[80]{0:T(128)S(1)}, s32[80]{0:T(128)}, u32[]{:S(2)}) copy-start(s32[80]{0:T(128)} %param.17) | copy-start | bytes 964
  10.2 11.7 %copy-start.5 = (f32[2048]{0:T(1024)S(1)}, f32[2048]{0:T(1024)}, u32[]{:S(2)}) copy-start(f32[2048]{0:T(1024)} %param.10) | copy-start | bytes 24580
  10.2 26.0 %all-to-all-start = ((bf16[5,16,64,128]{3,2,0,1:T(8,128)(2,1)}), bf16[5,16,64,128]{3,2,0,1:T(8,128)(2,1)S(1)}, u32[]{:S(2)}, u32[]{:S(2)}) async-start(bf16[5,16,64,128]{3,2,0,1:T(8,128)(2,1)} %copy.27), calls=%async_computation | async-start | bytes 2621440 | tf_op jit(solution)/shard_map/all_to_all | solution.py:72
  19.2 2.8 %copy-start.1 = (bf16[768,2048]{1,0:T(8,128)(2,1)S(1)}, bf16[768,2048]{1,0:T(8,128)(2,1)}, u32[]{:S(2)}) copy-start(bf16[768,2048]{1,0:T(8,128)(2,1)} %param.9) | copy-start | bytes 9437188
  22.0 17.7 %copy-start.4 = (s32[80]{0:T(128)S(1)}, s32[80]{0:T(128)}, u32[]{:S(2)}) copy-start(s32[80]{0:T(128)} %param.16) | copy-start | bytes 964
  36.2 9.9 %collective-permute-start = (bf16[5,16,64,128]{3,2,0,1:T(8,128)(2,1)S(1)}, bf16[5,16,64,128]{3,2,0,1:T(8,128)(2,1)}, u32[]{:S(2)}, u32[]{:S(2)}) collective-permute-start(bf16[5,16,64,128]{3,2,0,1:T(8,128)(2,1)S(1)} %all-to-all-done), channel_id=1, source_target_pairs={{0,1},{1,0},{2,3},{3,2},{4,5},{5,4},{6,7},{7,6},{8,9},{9,8},{10,11... | collective-permute-start | bytes 3932168 | tf_op jit(solution)/shard_map/ppermute | solution.py:74
  42.1 2.8 %copy-start.2 = (bf16[768,2048]{1,0:T(8,128)(2,1)S(1)}, bf16[768,2048]{1,0:T(8,128)(2,1)}, u32[]{:S(2)}) copy-start(bf16[768,2048]{1,0:T(8,128)(2,1)} %param.9) | copy-start | bytes 9437188
  96.2 1.8 %collective-permute-start.1 = (bf16[768,256]{1,0:T(8,128)(2,1)S(1)}, bf16[768,256]{1,0:T(8,128)(2,1)S(1)}, u32[]{:S(2)}, u32[]{:S(2)}) collective-permute-start(bf16[768,256]{1,0:T(8,128)(2,1)S(1)} %shard_map.91), channel_id=1, source_target_pairs={{0,1},{1,0},{2,3},{3,2},{4,5},{5,4},{6,7},{7,6},{8,9},{9,8},{10,11... | collective-permute-start | bytes 1179656 | tf_op jit(solution)/shard_map/ppermute | solution.py:101
  99.4 25.6 %all-to-all-start.1 = ((bf16[4,384,512]{2,1,0:T(8,128)(2,1)}), bf16[4,384,512]{2,1,0:T(8,128)(2,1)}, u32[]{:S(2)}, u32[]{:S(2)}) async-start(bf16[4,384,512]{2,1,0:T(8,128)(2,1)} %broadcast_in_dim.24), calls=%async_computation.1 | async-start | bytes 3145728 | tf_op jit(solution)/shard_map/all_to_all | solution.py:111
  128.0 2.5 %collective-permute-start.2 = (bf16[384,256]{1,0:T(8,128)(2,1)S(1)}, bf16[384,256]{1,0:T(8,128)(2,1)S(1)}, u32[]{:S(2)}, u32[]{:S(2)}) collective-permute-start(bf16[384,256]{1,0:T(8,128)(2,1)S(1)} %get-tuple-element.8), channel_id=1, source_target_pairs={{0,1},{1,0},{2,3},{3,2},{4,5},{5,4},{6,7},{7,6},{8,9},{9,8},{10,11... | collective-permute-start | bytes 589832 | tf_op jit(solution)/shard_map/ppermute | solution.py:121

commit v3 on v2

--- a/solution.py
+++ b/solution.py
@@ -125,7 +125,7 @@
     return projected
 
 
-BLOCK_ROWS = 128
+BLOCK_ROWS = 64
 
 
 def attend_kernel(window, bounds_ref, q_ref, *refs):
@@ -145,8 +145,7 @@
         r_first = r_first + (bounds_ref[request_count + k] <= first_row).astype(jnp.int32)
         r_last = r_last + (bounds_ref[k] < first_row + block_rows).astype(jnp.int32)
     r_last = jnp.minimum(r_last, request_count - 1)
-    column = lax.broadcasted_iota(jnp.int32, (stacked, row_count), 1)
-    fresh = fresh_ref[...]
+    half_count = row_count // 2
 
     def scores_of(keys):
         return lax.dot_general(
@@ -156,6 +155,20 @@
     def one_request(r, out_acc):
         begin = bounds_ref[r]
         finish = bounds_ref[request_count + r]
+        last_needed = jnp.minimum(finish, first_row + block_rows)
+        branch = jnp.where(
+            last_needed <= half_count, 0, jnp.where(begin >= half_count, 1, 2)
+        ).astype(jnp.int32)
+        branches = [
+            functools.partial(request_terms, 0, half_count),
+            functools.partial(request_terms, half_count, row_count),
+            functools.partial(request_terms, 0, row_count),
+        ]
+        return lax.switch(branch, branches, r, begin, finish, out_acc)
+
+    def request_terms(low, high, r, begin, finish, out_acc):
+        fresh = fresh_ref[low:high, :]
+        column = low + lax.broadcasted_iota(jnp.int32, (stacked, high - low), 1)
         in_request = (rows >= begin) & (rows < finish)
         threshold = jnp.where(in_request, rows - begin + 1, window)
         newest = jnp.where(in_request, rows, -1)

time: 132 us -> 113 us (0.86)
  Pallas kernels: 48.7 us -> 29.5 us
    pallas_call x1, Pallas kernels: 48.7 us -> 29.5 us  [attend(): pl.pallas_call(functools.partial(attend_kernel, window), out_shape=jax.Sh...]
  transfers between devices with their start and end apart: 5 -> 5, of which waited for: 4 -> 4; matrix products, arithmetic and copies ran while one was open for 13% -> 15% of each run, Pallas kernels for 0% -> 0%
where the time goes in v3:
time: 113 us; the launch traced here: 112 us
  waiting for transfers between devices  31.1 us (28%)
  Pallas kernels  29.5 us (26%)
  local copies, waits for them, and re-layouts  20.1 us (18%)
  starting transfers between devices  17.7 us (16%)
  matrix products  7.42 us (7%)
  other arithmetic  6.13 us (5%)
    pallas_call x1, Pallas kernels, attend(): pl.pallas_call(functools.partial(attend_kernel, window), out_shape=jax.Sh...  29.5 us
    all_to_all x1, waiting for transfers between devices, layer(): chips_heads = lax.all_to_all(sent, 'tz', 0, 0, tiled=True)  17.5 us
    all_to_all x1, waiting for transfers between devices, layer(): incoming = lax.all_to_all(outgoing, 'seq', 1, 1, tiled=True)  10.8 us
    all_to_all x1, starting transfers between devices, layer(): incoming = lax.all_to_all(outgoing, 'seq', 1, 1, tiled=True)  7.7 us
    gather x4, local copies, waits for them, and re-layouts, layer(): outgoing = head_pages[held_slot[all_groups].T]  5.66 us
    all_to_all x1, starting transfers between devices, layer(): chips_heads = lax.all_to_all(sent, 'tz', 0, 0, tiled=True)  5.04 us
    ppermute x1, starting transfers between devices, layer(): partner = lax.ppermute(incoming, 'tc', [(0, 1), (1, 0)])  3.49 us
    dot_general x1, matrix products, layer(): jnp.dot(normed, query_weight, preferred_element_type=jnp.float32)  3.33 us
  transfers between devices with their start and end apart: 5, of which 4 were waited for; matrix products, arithmetic and copies ran while one was open for 15% of the time, Pallas kernels for 0%

profile of v3, /device:TPU:1, one launch (start us, length us, event | category | flops | bytes accessed | tf_op | source)
XLA Modules:
  0.0 112.2 jit_solution(1701852468339757191)
XLA Ops:
  0.0 0.9 add_select_fusion.1
  0.9 0.7 reshape.164
  1.8 0.9 fusion.10
  2.7 1.2 %gather_fusion = s32[80]{0:T(128)S(1)} fusion(s32[16]{0:T(128)S(1)} %fusion.10, s32[1024]{0:T(1024)S(1)} %pad_clamp_fusion.2), kind=kCustom, calls=%fused_computation | custom fusion | bytes 960 | tf_op jit(solution)/shard_map/gather | solution.py:71
  4.2 1.7 %dynamic-slice_bitcast_fusion = bf16[64,64,128]{2,1,0:T(8,128)(2,1)S(1)} fusion(bf16[64,4,128,128]{3,2,1,0:T(8,128)(2,1)} %param.14, s32[]{:T(128)S(6)} %select_n.96, s32[]{:T(128)S(6)} %select_n.98), kind=kLoop, calls=%fused_computation.12 | loop fusion | bytes 2097160 | tf_op jit(solution)/shard_map/dynamic_slice | solution.py:70
  5.9 1.9 %gather_fusion.1 = bf16[80,64,128]{2,1,0:T(8,128)(2,1)} fusion(bf16[64,64,128]{2,1,0:T(8,128)(2,1)S(1)} %dynamic-slice_bitcast_fusion, s32[1024]{0:T(1024)S(1)} %pad_clamp_fusion.1), kind=kCustom, calls=%fused_computation.1 | custom fusion | bytes 2621760 | tf_op jit(solution)/shard_map/gather | solution.py:71
  7.7 2.5 %copy.27 = bf16[5,16,64,128]{3,2,0,1:T(8,128)(2,1)} copy(bf16[5,16,64,128]{3,2,1,0:T(8,128)(2,1)} %bitcast.29) | data formatting | bytes 2621440 | tf_op jit(solution)/shard_map/gather | solution.py:71
  10.2 7.7 %all-to-all-start = ((bf16[5,16,64,128]{3,2,0,1:T(8,128)(2,1)}), bf16[5,16,64,128]{3,2,0,1:T(8,128)(2,1)S(1)}, u32[]{:S(2)}, u32[]{:S(2)}) async-start(bf16[5,16,64,128]{3,2,0,1:T(8,128)(2,1)} %copy.27), calls=%async_computation | async-start | bytes 2621440 | tf_op jit(solution)/shard_map/all_to_all | solution.py:72
  18.0 0.1 select_reduce_fusion
  18.2 0.6 gather_fusion.2
  19.2 2.7 %fusion = f32[768]{0:T(1024)S(1)} fusion(bf16[768,2048]{1,0:T(8,128)(2,1)} %param.9), kind=kLoop, calls=%fused_computation.5 | loop fusion | flops 4717824 | bytes 3148800 | tf_op jit(solution)/shard_map/reduce_sum | solution.py:25
  22.0 3.3 %convolution_convert_fusion = bf16[768,256]{0,1:T(8,128)(2,1)} fusion(bf16[2048,256]{1,0:T(8,128)(2,1)} %param.11, bf16[768,2048]{1,0:T(8,128)(2,1)S(1)} %copy-done.1, f32[2048]{0:T(1024)S(1)} %copy-done.5, f32[768]{0:T(1024)S(1)} %add_rsqrt_fusion), kind=kOutput, calls=%fused_computation.10 | convolution fusion | flops 811794432 | bytes 4598784 | tf_op jit(solution)/shard_map/dot_general | solution.py:49
  25.3 10.8 %all-to-all-done = bf16[5,16,64,128]{3,2,0,1:T(8,128)(2,1)S(1)} async-done(((bf16[5,16,64,128]{3,2,0,1:T(8,128)(2,1)}), bf16[5,16,64,128]{3,2,0,1:T(8,128)(2,1)S(1)}, u32[]{:S(2)}, u32[]{:S(2)}) %all-to-all-start) | async-done | bytes 1310752 | tf_op jit(solution)/shard_map/all_to_all | solution.py:72
  36.2 3.5 %collective-permute-start = (bf16[5,16,64,128]{3,2,0,1:T(8,128)(2,1)S(1)}, bf16[5,16,64,128]{3,2,0,1:T(8,128)(2,1)}, u32[]{:S(2)}, u32[]{:S(2)}) collective-permute-start(bf16[5,16,64,128]{3,2,0,1:T(8,128)(2,1)S(1)} %all-to-all-done), channel_id=1, source_target_pairs={{0,1},{1,0},{2,3},{3,2},{4,5},{5,4},{6,7},{7,6},{8,9},{9,8},{10,11... | collective-permute-start | bytes 3932168 | tf_op jit(solution)/shard_map/ppermute | solution.py:74
  39.8 0.2 reduce-window.9
  39.9 2.2 %copy.25 = bf16[768,4,64]{2,0,1:T(8,128)(2,1)} copy(bf16[768,4,64]{0,2,1:T(8,128)(2,1)} %bitcast.31) | data formatting | bytes 786432 | tf_op jit(solution)/shard_map/reshape | solution.py:52
  42.3 1.4 %pad_bitcast_fusion.q_ref = bf16[4,768,128]{2,1,0:T(8,128)(2,1)S(1)} fusion(bf16[768,4,64]{2,0,1:T(8,128)(2,1)} %copy.25), kind=kLoop, calls=%fused_computation.17 | loop fusion | bytes 1179648 | tf_op jit(solution)/shard_map/transpose | solution.py:96
  43.7 1.1 %constant_dynamic-slice_fusion.3 = bf16[2048,1,128]{2,1,0:T(2,128)(2,1)S(1)} fusion(bf16[2048,4,128]{2,1,0:T(4,128)(2,1)S(1)} %copy-done, s32[]{:T(128)S(6)} %select_n.95), kind=kLoop, calls=%fused_computation.50 | loop fusion | bytes 1048580 | tf_op jit(solution)/shard_map/jit(dynamic_index_in_dim)/dynamic_slice | solution.py:53
  44.9 1.0 convolution_convert_fusion.1.refs_4_
  46.0 0.1 copy.28
  46.1 1.4 %copy.29 = bf16[5,16,64,128]{3,2,1,0:T(8,128)(2,1)S(1)} copy(bf16[5,16,64,128]{3,2,0,1:T(8,128)(2,1)} %collective-permute-done) | data formatting | bytes 2621440 | tf_op jit(solution)/shard_map/ppermute | solution.py:74
  47.5 29.5 %shard_map.91 = bf16[768,256]{1,0:T(8,128)(2,1)S(1)} custom-call(s32[10]{0:T(128)S(1)} %pad_add_fusion.bounds_ref, bf16[4,768,128]{2,1,0:T(8,128)(2,1)S(1)} %pad_bitcast_fusion.q_ref, bf16[5,1024,128]{2,1,0:T(8,128)(2,1)S(1)} %bitcast.27, s32[5,1,1024]{2,1,0:T(1,128)S(1)} %get-tuple-element.10.refs_1_, bf16[5,1024,128]{2,1,0:T(8,128)(2,1)S(1)} %bitcast.28, ...), custom_call_target="tpu_custom_call" | custom-call | tf_op jit(solution)/shard_map/pallas_call | solution.py:215
  77.0 0.1 collective-permute-start.1
  77.1 1.7 %collective-permute-done.1 = bf16[768,256]{1,0:T(8,128)(2,1)S(1)} collective-permute-done((bf16[768,256]{1,0:T(8,128)(2,1)S(1)}, bf16[768,256]{1,0:T(8,128)(2,1)S(1)}, u32[]{:S(2)}, u32[]{:S(2)}) %collective-permute-start.1) | collective-permute-done | bytes 393248 | tf_op jit(solution)/shard_map/ppermute | solution.py:101
  78.9 1.3 %broadcast_in_dim.24 = bf16[4,384,512]{2,1,0:T(8,128)(2,1)} broadcast(bf16[384,512]{1,0:T(8,128)(2,1)S(1)} %fusion.7), dimensions={1,2} | broadcast | bytes 1966080 | tf_op jit(solution)/shard_map/broadcast_in_dim | solution.py:110
  80.2 5.0 %all-to-all-start.1 = ((bf16[4,384,512]{2,1,0:T(8,128)(2,1)}), bf16[4,384,512]{2,1,0:T(8,128)(2,1)}, u32[]{:S(2)}, u32[]{:S(2)}) async-start(bf16[4,384,512]{2,1,0:T(8,128)(2,1)} %broadcast_in_dim.24), calls=%async_computation.1 | async-start | bytes 3145728 | tf_op jit(solution)/shard_map/all_to_all | solution.py:111
  85.2 3.1 %constant_dynamic-slice_fusion.2 = bf16[2048,512]{1,0:T(8,128)(2,1)} fusion(bf16[2048,2048]{1,0:T(8,128)(2,1)} %param.13, s32[]{:T(128)S(6)} %select_n.109), kind=kLoop, calls=%fused_computation.49 | loop fusion | bytes 4194308 | tf_op jit(solution)/shard_map/dynamic_slice | solution.py:113
  88.3 17.5 %all-to-all-done.1 = bf16[4,384,512]{2,1,0:T(8,128)(2,1)} async-done(((bf16[4,384,512]{2,1,0:T(8,128)(2,1)}), bf16[4,384,512]{2,1,0:T(8,128)(2,1)}, u32[]{:S(2)}, u32[]{:S(2)}) %all-to-all-start.1) | async-done | bytes 1572896 | tf_op jit(solution)/shard_map/all_to_all | solution.py:111
  105.8 3.0 %fusion.3 = bf16[384,512]{1,0:T(8,128)(2,1)S(1)} fusion(bf16[4,384,512]{2,1,0:T(8,128)(2,1)} %all-to-all-done.1, bf16[4,512,512]{2,1,0:T(8,128)(2,1)} %bitcast.30), kind=kOutput, calls=%fused_computation.9 | convolution fusion | flops 805502976 | bytes 4063232 | tf_op jit(solution)/shard_map/zrj,zjn->rn/dot_general | solution.py:115
  108.9 1.4 %collective-permute-start.2 = (bf16[384,256]{1,0:T(8,128)(2,1)S(1)}, bf16[384,256]{1,0:T(8,128)(2,1)S(1)}, u32[]{:S(2)}, u32[]{:S(2)}) collective-permute-start(bf16[384,256]{1,0:T(8,128)(2,1)S(1)} %get-tuple-element.8), channel_id=1, source_target_pairs={{0,1},{1,0},{2,3},{3,2},{4,5},{5,4},{6,7},{7,6},{8,9},{9,8},{10,11... | collective-permute-start | bytes 589832 | tf_op jit(solution)/shard_map/ppermute | solution.py:121
  110.3 1.1 collective-permute-done.2
  111.3 0.9 maximum_select_fusion
  (37 shorter events, 1.4 us)
Async XLA Ops:
  0.0 43.7 %copy-start = (bf16[2048,4,128]{2,1,0:T(4,128)(2,1)S(1)}, bf16[2048,4,128]{2,1,0:T(4,128)(2,1)}, u32[]{:S(2)}) copy-start(bf16[2048,4,128]{2,1,0:T(4,128)(2,1)} %param.12) | copy-start | bytes 6291460
  7.7 10.2 %copy-start.3 = (s32[80]{0:T(128)S(1)}, s32[80]{0:T(128)}, u32[]{:S(2)}) copy-start(s32[80]{0:T(128)} %param.17) | copy-start | bytes 964
  10.2 11.7 %copy-start.5 = (f32[2048]{0:T(1024)S(1)}, f32[2048]{0:T(1024)}, u32[]{:S(2)}) copy-start(f32[2048]{0:T(1024)} %param.10) | copy-start | bytes 24580
  10.2 26.0 %all-to-all-start = ((bf16[5,16,64,128]{3,2,0,1:T(8,128)(2,1)}), bf16[5,16,64,128]{3,2,0,1:T(8,128)(2,1)S(1)}, u32[]{:S(2)}, u32[]{:S(2)}) async-start(bf16[5,16,64,128]{3,2,0,1:T(8,128)(2,1)} %copy.27), calls=%async_computation | async-start | bytes 2621440 | tf_op jit(solution)/shard_map/all_to_all | solution.py:72
  19.2 2.8 %copy-start.1 = (bf16[768,2048]{1,0:T(8,128)(2,1)S(1)}, bf16[768,2048]{1,0:T(8,128)(2,1)}, u32[]{:S(2)}) copy-start(bf16[768,2048]{1,0:T(8,128)(2,1)} %param.9) | copy-start | bytes 9437188
  22.0 17.7 %copy-start.4 = (s32[80]{0:T(128)S(1)}, s32[80]{0:T(128)}, u32[]{:S(2)}) copy-start(s32[80]{0:T(128)} %param.16) | copy-start | bytes 964
  36.2 9.9 %collective-permute-start = (bf16[5,16,64,128]{3,2,0,1:T(8,128)(2,1)S(1)}, bf16[5,16,64,128]{3,2,0,1:T(8,128)(2,1)}, u32[]{:S(2)}, u32[]{:S(2)}) collective-permute-start(bf16[5,16,64,128]{3,2,0,1:T(8,128)(2,1)S(1)} %all-to-all-done), channel_id=1, source_target_pairs={{0,1},{1,0},{2,3},{3,2},{4,5},{5,4},{6,7},{7,6},{8,9},{9,8},{10,11... | collective-permute-start | bytes 3932168 | tf_op jit(solution)/shard_map/ppermute | solution.py:74
  42.1 2.8 %copy-start.2 = (bf16[768,2048]{1,0:T(8,128)(2,1)S(1)}, bf16[768,2048]{1,0:T(8,128)(2,1)}, u32[]{:S(2)}) copy-start(bf16[768,2048]{1,0:T(8,128)(2,1)} %param.9) | copy-start | bytes 9437188
  77.0 1.8 %collective-permute-start.1 = (bf16[768,256]{1,0:T(8,128)(2,1)S(1)}, bf16[768,256]{1,0:T(8,128)(2,1)S(1)}, u32[]{:S(2)}, u32[]{:S(2)}) collective-permute-start(bf16[768,256]{1,0:T(8,128)(2,1)S(1)} %shard_map.91), channel_id=1, source_target_pairs={{0,1},{1,0},{2,3},{3,2},{4,5},{5,4},{6,7},{7,6},{8,9},{9,8},{10,11... | collective-permute-start | bytes 1179656 | tf_op jit(solution)/shard_map/ppermute | solution.py:101
  80.2 25.6 %all-to-all-start.1 = ((bf16[4,384,512]{2,1,0:T(8,128)(2,1)}), bf16[4,384,512]{2,1,0:T(8,128)(2,1)}, u32[]{:S(2)}, u32[]{:S(2)}) async-start(bf16[4,384,512]{2,1,0:T(8,128)(2,1)} %broadcast_in_dim.24), calls=%async_computation.1 | async-start | bytes 3145728 | tf_op jit(solution)/shard_map/all_to_all | solution.py:111
  108.9 2.5 %collective-permute-start.2 = (bf16[384,256]{1,0:T(8,128)(2,1)S(1)}, bf16[384,256]{1,0:T(8,128)(2,1)S(1)}, u32[]{:S(2)}, u32[]{:S(2)}) collective-permute-start(bf16[384,256]{1,0:T(8,128)(2,1)S(1)} %get-tuple-element.8), channel_id=1, source_target_pairs={{0,1},{1,0},{2,3},{3,2},{4,5},{5,4},{6,7},{7,6},{8,9},{9,8},{10,11... | collective-permute-start | bytes 589832 | tf_op jit(solution)/shard_map/ppermute | solution.py:121

commit v4 on v2

--- a/solution.py
+++ b/solution.py
@@ -91,9 +91,7 @@
     starts = jnp.cumsum(lengths) - lengths
     bounds = jnp.concatenate([starts, starts + lengths]).astype(jnp.int32)
     fresh_pad = new_token_rows
-    query_pad = jnp.concatenate(
-        [query_rows, jnp.zeros_like(query_rows)], axis=-1
-    ).transpose(1, 0, 2)
+    query_pad = query_rows.transpose(1, 0, 2)
     attended = attend(bounds, query_pad, key_parts, fresh_pad, WINDOW_LENGTH)
     swap = [(0, 1), (1, 0)]
     z_count = lax.axis_size("tz")
@@ -125,19 +123,30 @@
     return projected
 
 
-BLOCK_ROWS = 128
-
-
-def attend_kernel(window, bounds_ref, q_ref, *refs):
-    part_refs = list(zip(refs[0:-2:2], refs[1:-2:2]))
-    fresh_ref, o_ref = refs[-2], refs[-1]
+BLOCK_ROWS = 64
+
+
+def attend_kernel(window, part_count, bounds_ref, q_ref, *refs):
+    part_refs = list(zip(refs[0 : 2 * part_count : 2], refs[1 : 2 * part_count : 2]))
+    fresh_ref, o_ref, fresh_t_ref = refs[2 * part_count : 2 * part_count + 3]
+    key_t_refs = refs[2 * part_count + 3 :]
     heads, block_rows, _ = q_ref.shape
     stacked = heads * block_rows
     request_count = part_refs[0][0].shape[0]
     row_count = fresh_ref.shape[0]
     first_row = pl.program_id(0) * block_rows
     score_scale = HEAD_SIZE ** (-0.5)
-    q = q_ref[...].reshape(stacked, 2 * HEAD_SIZE)
+    q = q_ref[...].reshape(stacked, HEAD_SIZE)
+
+    @pl.when(pl.program_id(0) == 0)
+    def _():
+        fresh_t_ref[...] = fresh_ref[:, :HEAD_SIZE].astype(jnp.float32).T.astype(jnp.bfloat16)
+        for (keys_ref, _), key_t_ref in zip(part_refs, key_t_refs):
+            for r in range(request_count):
+                key_t_ref[r] = (
+                    keys_ref[r][:, :HEAD_SIZE].astype(jnp.float32).T.astype(jnp.bfloat16)
+                )
+
     rows = first_row + lax.broadcasted_iota(jnp.int32, (heads, block_rows, 1), 1).reshape(stacked, 1)
     r_first = jnp.int32(0)
     r_last = jnp.int32(-1)
@@ -148,10 +157,8 @@
     column = lax.broadcasted_iota(jnp.int32, (stacked, row_count), 1)
     fresh = fresh_ref[...]
 
-    def scores_of(keys):
-        return lax.dot_general(
-            q, keys, (((1,), (1,)), ((), ())), preferred_element_type=jnp.float32
-        ) * score_scale
+    def scores_of(keys_t):
+        return jnp.dot(q, keys_t, preferred_element_type=jnp.float32) * score_scale
 
     def one_request(r, out_acc):
         begin = bounds_ref[r]
@@ -162,10 +169,10 @@
         suffix_mask = (
             (column >= begin) & (column <= newest) & (rows - column < WINDOW_LENGTH)
         )
-        pieces = [(fresh, scores_of(fresh), suffix_mask)]
-        for keys_ref, positions_ref in part_refs:
+        pieces = [(fresh, scores_of(fresh_t_ref[...]), suffix_mask)]
+        for (keys_ref, positions_ref), key_t_ref in zip(part_refs, key_t_refs):
             keys = keys_ref[r]
-            pieces.append((keys, scores_of(keys), positions_ref[r] >= threshold))
+            pieces.append((keys, scores_of(key_t_ref[r]), positions_ref[r] >= threshold))
         top = jnp.full((stacked, 1), MASKED_SCORE, jnp.float32)
         for _, scores, mask in pieces:
             top = jnp.maximum(
@@ -200,15 +207,20 @@
         part_specs.append(pl.BlockSpec(positions.shape, lambda i, b: (0, 0, 0)))
         part_args.extend([keys, positions])
     return pl.pallas_call(
-        functools.partial(attend_kernel, window),
+        functools.partial(attend_kernel, window, len(key_parts)),
         out_shape=jax.ShapeDtypeStruct((row_count, heads * HEAD_SIZE), jnp.bfloat16),
         grid_spec=pltpu.PrefetchScalarGridSpec(
             num_scalar_prefetch=1,
             grid=(row_count // block_rows,),
             in_specs=[pl.BlockSpec((heads, block_rows, width), lambda i, b: (0, i, 0))]
             + part_specs
-            + [pl.BlockSpec((row_count, width), lambda i, b: (0, 0))],
+            + [pl.BlockSpec(fresh_rows.shape, lambda i, b: (0, 0))],
             out_specs=pl.BlockSpec((block_rows, heads * HEAD_SIZE), lambda i, b: (i, 0)),
+            scratch_shapes=[pltpu.VMEM((HEAD_SIZE, fresh_rows.shape[0]), jnp.bfloat16)]
+            + [
+                pltpu.VMEM((keys.shape[0], HEAD_SIZE, keys.shape[1]), jnp.bfloat16)
+                for keys, _ in key_parts
+            ],
         ),
         compiler_params=pltpu.CompilerParams(
             dimension_semantics=("arbitrary",), vmem_limit_bytes=48 * 1024 * 1024

time: 132 us -> 120 us (0.909)
  Pallas kernels: 48.7 us -> 33.9 us
  waiting for transfers between devices: 31.1 us -> 34.5 us
  local copies, waits for them, and re-layouts: 20.1 us -> 18.1 us
  matrix products: 7.42 us -> 9.39 us
    pallas_call x1, Pallas kernels: 48.7 us -> 33.9 us  [attend(): pl.pallas_call(functools.partial(attend_kernel, window, len(key_parts)),...]
    all_to_all x1, waiting for transfers between devices: 10.8 us -> 14.2 us  [layer(): incoming = lax.all_to_all(outgoing, 'seq', 1, 1, tiled=True)]
    dot_general x1, matrix products: 1.04 us -> 2.93 us  [layer(): jnp.dot(normed, head_weight, preferred_element_type=jnp.float32)]
    reshape x1, local copies, waits for them, and re-layouts: 2.18 us -> 0.37 us  [layer(): query_rows = query_rows.reshape(row_count, resident_heads, HEAD_SIZE)]
    transpose x1 -> x0, local copies, waits for them, and re-layouts: 1.44 us -> none  [layer(): query_pad = jnp.concatenate([query_rows, jnp.zeros_like(query_rows)], axi...]
  transfers between devices with their start and end apart: 5 -> 5, of which waited for: 4 -> 4; matrix products, arithmetic and copies ran while one was open for 13% -> 14% of each run, Pallas kernels for 0% -> 0%
where the time goes in v4:
time: 120 us
  waiting for transfers between devices  34.5 us (29%)
  Pallas kernels  33.9 us (28%)
  local copies, waits for them, and re-layouts  18.1 us (15%)
  starting transfers between devices  17.8 us (15%)
  matrix products  9.39 us (8%)
  other arithmetic  5.99 us (5%)
    pallas_call x1, Pallas kernels, attend(): pl.pallas_call(functools.partial(attend_kernel, window, len(key_parts)),...  33.9 us
    all_to_all x1, waiting for transfers between devices, layer(): chips_heads = lax.all_to_all(sent, 'tz', 0, 0, tiled=True)  17.5 us
    all_to_all x1, waiting for transfers between devices, layer(): incoming = lax.all_to_all(outgoing, 'seq', 1, 1, tiled=True)  14.2 us
    all_to_all x1, starting transfers between devices, layer(): incoming = lax.all_to_all(outgoing, 'seq', 1, 1, tiled=True)  7.75 us
    gather x4, local copies, waits for them, and re-layouts, layer(): outgoing = head_pages[held_slot[all_groups].T]  5.67 us
    all_to_all x1, starting transfers between devices, layer(): chips_heads = lax.all_to_all(sent, 'tz', 0, 0, tiled=True)  5.02 us
    ppermute x1, starting transfers between devices, layer(): partner = lax.ppermute(incoming, 'tc', [(0, 1), (1, 0)])  3.49 us
    dot_general x1, matrix products, layer(): jnp.dot(normed, query_weight, preferred_element_type=jnp.float32)  3.43 us
  transfers between devices with their start and end apart: 5, of which 4 were waited for; matrix products, arithmetic and copies ran while one was open for 14% of the time, Pallas kernels for 0%

profile of v4, /device:TPU:1, one launch (start us, length us, event | category | flops | bytes accessed | tf_op | source)
XLA Modules:
  0.0 119.8 jit_solution(5377716524098743501)
XLA Ops:
  0.0 0.9 add_select_fusion.1
  0.9 0.7 reshape.164
  1.8 0.9 fusion.10
  2.7 1.2 %gather_fusion = s32[80]{0:T(128)S(1)} fusion(s32[16]{0:T(128)S(1)} %fusion.10, s32[1024]{0:T(1024)S(1)} %pad_clamp_fusion.2), kind=kCustom, calls=%fused_computation | custom fusion | bytes 960 | tf_op jit(solution)/shard_map/gather | solution.py:71
  4.2 1.7 %dynamic-slice_bitcast_fusion = bf16[64,64,128]{2,1,0:T(8,128)(2,1)S(1)} fusion(bf16[64,4,128,128]{3,2,1,0:T(8,128)(2,1)} %param.14, s32[]{:T(128)S(6)} %select_n.96, s32[]{:T(128)S(6)} %select_n.98), kind=kLoop, calls=%fused_computation.12 | loop fusion | bytes 2097160 | tf_op jit(solution)/shard_map/dynamic_slice | solution.py:70
  5.9 1.9 %gather_fusion.1 = bf16[80,64,128]{2,1,0:T(8,128)(2,1)} fusion(bf16[64,64,128]{2,1,0:T(8,128)(2,1)S(1)} %dynamic-slice_bitcast_fusion, s32[1024]{0:T(1024)S(1)} %pad_clamp_fusion.1), kind=kCustom, calls=%fused_computation.1 | custom fusion | bytes 2621760 | tf_op jit(solution)/shard_map/gather | solution.py:71
  7.7 2.5 %copy.27 = bf16[5,16,64,128]{3,2,0,1:T(8,128)(2,1)} copy(bf16[5,16,64,128]{3,2,1,0:T(8,128)(2,1)} %bitcast.29) | data formatting | bytes 2621440 | tf_op jit(solution)/shard_map/gather | solution.py:71
  10.2 7.7 %all-to-all-start = ((bf16[5,16,64,128]{3,2,0,1:T(8,128)(2,1)}), bf16[5,16,64,128]{3,2,0,1:T(8,128)(2,1)}, u32[]{:S(2)}, u32[]{:S(2)}) async-start(bf16[5,16,64,128]{3,2,0,1:T(8,128)(2,1)} %copy.27), calls=%async_computation | async-start | bytes 2621440 | tf_op jit(solution)/shard_map/all_to_all | solution.py:72
  18.1 0.1 select_reduce_fusion
  18.2 0.6 gather_fusion.2
  18.9 0.1 add.170
  19.3 0.2 reduce-window.9
  19.5 2.6 %fusion = f32[768]{0:T(1024)S(1)} fusion(bf16[768,2048]{1,0:T(8,128)(2,1)} %param.9), kind=kLoop, calls=%fused_computation.5 | loop fusion | flops 4717824 | bytes 3148800 | tf_op jit(solution)/shard_map/reduce_sum | solution.py:25
  22.1 14.2 %all-to-all-done = bf16[5,16,64,128]{3,2,0,1:T(8,128)(2,1)} async-done(((bf16[5,16,64,128]{3,2,0,1:T(8,128)(2,1)}), bf16[5,16,64,128]{3,2,0,1:T(8,128)(2,1)}, u32[]{:S(2)}, u32[]{:S(2)}) %all-to-all-start) | async-done | bytes 1310752 | tf_op jit(solution)/shard_map/all_to_all | solution.py:72
  36.3 3.5 %collective-permute-start = (bf16[5,16,64,128]{3,2,0,1:T(8,128)(2,1)}, bf16[5,16,64,128]{3,2,0,1:T(8,128)(2,1)}, u32[]{:S(2)}, u32[]{:S(2)}) collective-permute-start(bf16[5,16,64,128]{3,2,0,1:T(8,128)(2,1)} %all-to-all-done), channel_id=1, source_target_pairs={{0,1},{1,0},{2,3},{3,2},{4,5},{5,4},{6,7},{7,6},{8,9},{9,8},{10,11... | collective-permute-start | bytes 3932168 | tf_op jit(solution)/shard_map/ppermute | solution.py:74
  39.8 3.4 %convolution_convert_fusion = bf16[768,256]{0,1:T(8,128)(2,1)S(1)} fusion(bf16[2048,256]{1,0:T(8,128)(2,1)} %param.11, bf16[768,2048]{1,0:T(8,128)(2,1)} %param.9, f32[2048]{0:T(1024)S(1)} %copy-done.3, f32[768]{0:T(1024)S(1)} %add_rsqrt_fusion), kind=kOutput, calls=%fused_computation.10 | convolution fusion | flops 811794432 | bytes 4598784 | tf_op jit(solution)/shard_map/dot_general | solution.py:49
  43.2 0.4 copy.25
  43.8 1.1 constant_dynamic-slice_fusion.3
  44.9 2.9 %convolution_convert_fusion.1.refs_4_ = bf16[768,128]{1,0:T(8,128)(2,1)S(1)} fusion(bf16[768,2048]{1,0:T(8,128)(2,1)} %param.9, f32[2048]{0:T(1024)S(1)} %copy-done.3, f32[768]{0:T(1024)S(1)} %add_rsqrt_fusion, bf16[2048,1,128]{2,1,0:T(2,128)(2,1)S(1)} %constant_dynamic-slice_fusion.3), kind=kOutput, calls=%fused_computation.11 | convolution fusion | flops 409042944 | bytes 3877888 | tf_op jit(solution)/shard_map/dot_general | solution.py:54
  47.9 1.4 %copy.28 = bf16[5,16,64,128]{3,2,1,0:T(8,128)(2,1)S(1)} copy(bf16[5,16,64,128]{3,2,0,1:T(8,128)(2,1)} %all-to-all-done) | data formatting | bytes 2621440 | tf_op jit(solution)/shard_map/all_to_all | solution.py:72
  49.3 1.4 %copy.29 = bf16[5,16,64,128]{3,2,1,0:T(8,128)(2,1)S(1)} copy(bf16[5,16,64,128]{3,2,0,1:T(8,128)(2,1)} %collective-permute-done) | data formatting | bytes 2621440 | tf_op jit(solution)/shard_map/ppermute | solution.py:74
  50.7 33.9 %shard_map.91 = bf16[768,256]{1,0:T(8,128)(2,1)S(1)} custom-call(s32[10]{0:T(128)S(1)} %pad_add_fusion.bounds_ref, bf16[4,768,64]{2,1,0:T(8,128)(2,1)S(1)} %bitcast.28, bf16[5,1024,128]{2,1,0:T(8,128)(2,1)S(1)} %bitcast.26, s32[5,1,1024]{2,1,0:T(1,128)S(1)} %get-tuple-element.10.refs_1_, bf16[5,1024,128]{2,1,0:T(8,128)(2,1)S(1)} %bitcast.27, ...), custom_call_target="tpu_custom_call" | custom-call | tf_op jit(solution)/shard_map/pallas_call | solution.py:209
  84.7 1.7 %collective-permute-done.1 = bf16[768,256]{1,0:T(8,128)(2,1)S(1)} collective-permute-done((bf16[768,256]{1,0:T(8,128)(2,1)S(1)}, bf16[768,256]{1,0:T(8,128)(2,1)S(1)}, u32[]{:S(2)}, u32[]{:S(2)}) %collective-permute-start.1) | collective-permute-done | bytes 393248 | tf_op jit(solution)/shard_map/ppermute | solution.py:99
  86.4 0.1 fusion.7
  86.5 1.3 %broadcast_in_dim.38 = bf16[4,384,512]{2,1,0:T(8,128)(2,1)} broadcast(bf16[384,512]{1,0:T(8,128)(2,1)S(1)} %fusion.7), dimensions={1,2} | broadcast | bytes 1966080 | tf_op jit(solution)/shard_map/broadcast_in_dim | solution.py:108
  87.8 5.0 %all-to-all-start.1 = ((bf16[4,384,512]{2,1,0:T(8,128)(2,1)}), bf16[4,384,512]{2,1,0:T(8,128)(2,1)}, u32[]{:S(2)}, u32[]{:S(2)}) async-start(bf16[4,384,512]{2,1,0:T(8,128)(2,1)} %broadcast_in_dim.38), calls=%async_computation.1 | async-start | bytes 3145728 | tf_op jit(solution)/shard_map/all_to_all | solution.py:109
  92.8 3.1 %constant_dynamic-slice_fusion.2 = bf16[2048,512]{1,0:T(8,128)(2,1)} fusion(bf16[2048,2048]{1,0:T(8,128)(2,1)} %param.13, s32[]{:T(128)S(6)} %select_n.109), kind=kLoop, calls=%fused_computation.48 | loop fusion | bytes 4194308 | tf_op jit(solution)/shard_map/dynamic_slice | solution.py:111
  95.9 17.5 %all-to-all-done.1 = bf16[4,384,512]{2,1,0:T(8,128)(2,1)} async-done(((bf16[4,384,512]{2,1,0:T(8,128)(2,1)}), bf16[4,384,512]{2,1,0:T(8,128)(2,1)}, u32[]{:S(2)}, u32[]{:S(2)}) %all-to-all-start.1) | async-done | bytes 1572896 | tf_op jit(solution)/shard_map/all_to_all | solution.py:109
  113.4 3.0 %fusion.3 = bf16[384,512]{1,0:T(8,128)(2,1)S(1)} fusion(bf16[4,384,512]{2,1,0:T(8,128)(2,1)} %all-to-all-done.1, bf16[4,512,512]{2,1,0:T(8,128)(2,1)} %bitcast.30), kind=kOutput, calls=%fused_computation.9 | convolution fusion | flops 805502976 | bytes 4063232 | tf_op jit(solution)/shard_map/zrj,zjn->rn/dot_general | solution.py:113
  116.4 1.4 %collective-permute-start.2 = (bf16[384,256]{1,0:T(8,128)(2,1)S(1)}, bf16[384,256]{1,0:T(8,128)(2,1)S(1)}, u32[]{:S(2)}, u32[]{:S(2)}) collective-permute-start(bf16[384,256]{1,0:T(8,128)(2,1)S(1)} %get-tuple-element.8), channel_id=1, source_target_pairs={{0,1},{1,0},{2,3},{3,2},{4,5},{5,4},{6,7},{7,6},{8,9},{9,8},{10,11... | collective-permute-start | bytes 589832 | tf_op jit(solution)/shard_map/ppermute | solution.py:119
  117.9 1.1 collective-permute-done.2
  118.9 0.9 maximum_select_fusion
  (32 shorter events, 1.2 us)
Async XLA Ops:
  0.0 43.8 %copy-start = (bf16[2048,4,128]{2,1,0:T(4,128)(2,1)S(1)}, bf16[2048,4,128]{2,1,0:T(4,128)(2,1)}, u32[]{:S(2)}) copy-start(bf16[2048,4,128]{2,1,0:T(4,128)(2,1)} %param.12) | copy-start | bytes 6291460
  7.7 10.3 %copy-start.1 = (s32[80]{0:T(128)S(1)}, s32[80]{0:T(128)}, u32[]{:S(2)}) copy-start(s32[80]{0:T(128)} %param.17) | copy-start | bytes 964
  7.7 11.5 %copy-start.2 = (s32[80]{0:T(128)S(1)}, s32[80]{0:T(128)}, u32[]{:S(2)}) copy-start(s32[80]{0:T(128)} %param.16) | copy-start | bytes 964
  10.2 29.6 %copy-start.3 = (f32[2048]{0:T(1024)S(1)}, f32[2048]{0:T(1024)}, u32[]{:S(2)}) copy-start(f32[2048]{0:T(1024)} %param.10) | copy-start | bytes 24580
  10.2 26.1 %all-to-all-start = ((bf16[5,16,64,128]{3,2,0,1:T(8,128)(2,1)}), bf16[5,16,64,128]{3,2,0,1:T(8,128)(2,1)}, u32[]{:S(2)}, u32[]{:S(2)}) async-start(bf16[5,16,64,128]{3,2,0,1:T(8,128)(2,1)} %copy.27), calls=%async_computation | async-start | bytes 2621440 | tf_op jit(solution)/shard_map/all_to_all | solution.py:72
  36.3 13.0 %collective-permute-start = (bf16[5,16,64,128]{3,2,0,1:T(8,128)(2,1)}, bf16[5,16,64,128]{3,2,0,1:T(8,128)(2,1)}, u32[]{:S(2)}, u32[]{:S(2)}) collective-permute-start(bf16[5,16,64,128]{3,2,0,1:T(8,128)(2,1)} %all-to-all-done), channel_id=1, source_target_pairs={{0,1},{1,0},{2,3},{3,2},{4,5},{5,4},{6,7},{7,6},{8,9},{9,8},{10,11... | collective-permute-start | bytes 3932168 | tf_op jit(solution)/shard_map/ppermute | solution.py:74
  84.6 1.8 %collective-permute-start.1 = (bf16[768,256]{1,0:T(8,128)(2,1)S(1)}, bf16[768,256]{1,0:T(8,128)(2,1)S(1)}, u32[]{:S(2)}, u32[]{:S(2)}) collective-permute-start(bf16[768,256]{1,0:T(8,128)(2,1)S(1)} %shard_map.91), channel_id=1, source_target_pairs={{0,1},{1,0},{2,3},{3,2},{4,5},{5,4},{6,7},{7,6},{8,9},{9,8},{10,11... | collective-permute-start | bytes 1179656 | tf_op jit(solution)/shard_map/ppermute | solution.py:99
  87.8 25.5 %all-to-all-start.1 = ((bf16[4,384,512]{2,1,0:T(8,128)(2,1)}), bf16[4,384,512]{2,1,0:T(8,128)(2,1)}, u32[]{:S(2)}, u32[]{:S(2)}) async-start(bf16[4,384,512]{2,1,0:T(8,128)(2,1)} %broadcast_in_dim.38), calls=%async_computation.1 | async-start | bytes 3145728 | tf_op jit(solution)/shard_map/all_to_all | solution.py:109
  116.4 2.5 %collective-permute-start.2 = (bf16[384,256]{1,0:T(8,128)(2,1)S(1)}, bf16[384,256]{1,0:T(8,128)(2,1)S(1)}, u32[]{:S(2)}, u32[]{:S(2)}) collective-permute-start(bf16[384,256]{1,0:T(8,128)(2,1)S(1)} %get-tuple-element.8), channel_id=1, source_target_pairs={{0,1},{1,0},{2,3},{3,2},{4,5},{5,4},{6,7},{7,6},{8,9},{9,8},{10,11... | collective-permute-start | bytes 589832 | tf_op jit(solution)/shard_map/ppermute | solution.py:119

commit v5 on v4

--- a/solution.py
+++ b/solution.py
@@ -154,11 +154,8 @@
         r_first = r_first + (bounds_ref[request_count + k] <= first_row).astype(jnp.int32)
         r_last = r_last + (bounds_ref[k] < first_row + block_rows).astype(jnp.int32)
     r_last = jnp.minimum(r_last, request_count - 1)
-    column = lax.broadcasted_iota(jnp.int32, (stacked, row_count), 1)
-    fresh = fresh_ref[...]
-
-    def scores_of(keys_t):
-        return jnp.dot(q, keys_t, preferred_element_type=jnp.float32) * score_scale
+
+    chunk = 128
 
     def one_request(r, out_acc):
         begin = bounds_ref[r]
@@ -166,26 +163,57 @@
         in_request = (rows >= begin) & (rows < finish)
         threshold = jnp.where(in_request, rows - begin + 1, window)
         newest = jnp.where(in_request, rows, -1)
-        suffix_mask = (
-            (column >= begin) & (column <= newest) & (rows - column < WINDOW_LENGTH)
-        )
-        pieces = [(fresh, scores_of(fresh_t_ref[...]), suffix_mask)]
-        for (keys_ref, positions_ref), key_t_ref in zip(part_refs, key_t_refs):
-            keys = keys_ref[r]
-            pieces.append((keys, scores_of(key_t_ref[r]), positions_ref[r] >= threshold))
+        lane = lax.broadcasted_iota(jnp.int32, (1, chunk), 1)
+
+        def fresh_piece(c):
+            start = pl.multiple_of(c * chunk, chunk)
+            scores = jnp.dot(
+                q, fresh_t_ref[:, pl.ds(start, chunk)], preferred_element_type=jnp.float32
+            ) * score_scale
+            column = start + lane
+            mask = (column >= begin) & (column <= newest) & (rows - column < WINDOW_LENGTH)
+            return scores, mask, fresh_ref[pl.ds(start, chunk), :]
+
+        def part_piece(p, c):
+            keys_ref, positions_ref = part_refs[p]
+            start = pl.multiple_of(c * chunk, chunk)
+            scores = jnp.dot(
+                q, key_t_refs[p][r, :, pl.ds(start, chunk)], preferred_element_type=jnp.float32
+            ) * score_scale
+            mask = positions_ref[r, :, pl.ds(start, chunk)] >= threshold
+            return scores, mask, keys_ref[r, pl.ds(start, chunk), :]
+
+        piece_makers = [(fresh_piece, row_count // chunk)] + [
+            (functools.partial(part_piece, p), part_refs[p][0].shape[1] // chunk)
+            for p in range(len(part_refs))
+        ]
+
         top = jnp.full((stacked, 1), MASKED_SCORE, jnp.float32)
-        for _, scores, mask in pieces:
-            top = jnp.maximum(
-                top, jnp.max(jnp.where(mask, scores, MASKED_SCORE), axis=1, keepdims=True)
-            )
-        total = jnp.zeros_like(top)
+        for make, count in piece_makers:
+
+            def max_step(c, top, make=make):
+                scores, mask, _ = make(c)
+                return jnp.maximum(
+                    top, jnp.max(jnp.where(mask, scores, MASKED_SCORE), axis=1, keepdims=True)
+                )
+
+            top = lax.fori_loop(0, count, max_step, top)
+
+        total = jnp.zeros((stacked, 1), jnp.float32)
         weighted = jnp.zeros((stacked, 2 * HEAD_SIZE), jnp.float32)
-        for keys, scores, mask in pieces:
-            raw = jnp.where(mask, jnp.exp(scores - top), 0.0)
-            total = total + jnp.sum(raw, axis=1, keepdims=True)
-            weighted = weighted + jnp.dot(
-                raw.astype(jnp.bfloat16), keys, preferred_element_type=jnp.float32
-            )
+        for make, count in piece_makers:
+
+            def sum_step(c, carry, make=make):
+                total, weighted = carry
+                scores, mask, keys = make(c)
+                raw = jnp.where(mask, jnp.exp(scores - top), 0.0)
+                total = total + jnp.sum(raw, axis=1, keepdims=True)
+                weighted = weighted + jnp.dot(
+                    raw.astype(jnp.bfloat16), keys, preferred_element_type=jnp.float32
+                )
+                return total, weighted
+
+            total, weighted = lax.fori_loop(0, count, sum_step, (total, weighted))
         safe_total = jnp.where(in_request, total, 1.0)
         return jnp.where(in_request, weighted / safe_total, out_acc)
 

time: 120 us -> 280 us (2.33)
  Pallas kernels: 33.9 us -> 194 us
    pallas_call x1, Pallas kernels: 33.9 us -> 194 us  [attend(): pl.pallas_call(functools.partial(attend_kernel, window, len(key_parts)),...]
  transfers between devices with their start and end apart: 5 -> 5, of which waited for: 4 -> 4; matrix products, arithmetic and copies ran while one was open for 14% -> 6% of each run, Pallas kernels for 0% -> 0%
where the time goes in v5:
time: 280 us
  Pallas kernels  194 us (69%)
  waiting for transfers between devices  34.5 us (12%)
  local copies, waits for them, and re-layouts  18.1 us (6%)
  starting transfers between devices  17.8 us (6%)
  matrix products  9.39 us (3%)
  other arithmetic  5.99 us (2%)
    pallas_call x1, Pallas kernels, attend(): pl.pallas_call(functools.partial(attend_kernel, window, len(key_parts)),...  194 us
    all_to_all x1, waiting for transfers between devices, layer(): chips_heads = lax.all_to_all(sent, 'tz', 0, 0, tiled=True)  17.5 us
    all_to_all x1, waiting for transfers between devices, layer(): incoming = lax.all_to_all(outgoing, 'seq', 1, 1, tiled=True)  14.2 us
    all_to_all x1, starting transfers between devices, layer(): incoming = lax.all_to_all(outgoing, 'seq', 1, 1, tiled=True)  7.75 us
    gather x4, local copies, waits for them, and re-layouts, layer(): outgoing = head_pages[held_slot[all_groups].T]  5.67 us
  transfers between devices with their start and end apart: 5, of which 4 were waited for; matrix products, arithmetic and copies ran while one was open for 6% of the time, Pallas kernels for 0%

profile of v5, /device:TPU:1, one launch (start us, length us, event | category | flops | bytes accessed | tf_op | source)
XLA Modules:
  0.0 279.5 jit_solution(14738139044061239858)
XLA Ops:
  0.0 0.9 add_select_fusion.1
  0.9 0.7 reshape.164
  1.8 0.9 fusion.10
  2.7 1.2 gather_fusion
  4.2 1.7 dynamic-slice_bitcast_fusion
  5.9 1.9 gather_fusion.1
  7.7 2.5 copy.27
  10.2 7.7 %all-to-all-start = ((bf16[5,16,64,128]{3,2,0,1:T(8,128)(2,1)}), bf16[5,16,64,128]{3,2,0,1:T(8,128)(2,1)}, u32[]{:S(2)}, u32[]{:S(2)}) async-start(bf16[5,16,64,128]{3,2,0,1:T(8,128)(2,1)} %copy.27), calls=%async_computation | async-start | bytes 2621440 | tf_op jit(solution)/shard_map/all_to_all | solution.py:72
  18.1 0.1 select_reduce_fusion
  18.2 0.6 gather_fusion.2
  18.9 0.1 add.170
  19.0 0.1 add.180
  19.3 0.2 reduce-window.9
  19.5 2.6 fusion
  22.1 14.2 %all-to-all-done = bf16[5,16,64,128]{3,2,0,1:T(8,128)(2,1)} async-done(((bf16[5,16,64,128]{3,2,0,1:T(8,128)(2,1)}), bf16[5,16,64,128]{3,2,0,1:T(8,128)(2,1)}, u32[]{:S(2)}, u32[]{:S(2)}) %all-to-all-start) | async-done | bytes 1310752 | tf_op jit(solution)/shard_map/all_to_all | solution.py:72
  36.3 3.5 %collective-permute-start = (bf16[5,16,64,128]{3,2,0,1:T(8,128)(2,1)}, bf16[5,16,64,128]{3,2,0,1:T(8,128)(2,1)}, u32[]{:S(2)}, u32[]{:S(2)}) collective-permute-start(bf16[5,16,64,128]{3,2,0,1:T(8,128)(2,1)} %all-to-all-done), channel_id=1, source_target_pairs={{0,1},{1,0},{2,3},{3,2},{4,5},{5,4},{6,7},{7,6},{8,9},{9,8},{10,11... | collective-permute-start | bytes 3932168 | tf_op jit(solution)/shard_map/ppermute | solution.py:74
  39.8 3.4 %convolution_convert_fusion = bf16[768,256]{0,1:T(8,128)(2,1)S(1)} fusion(bf16[2048,256]{1,0:T(8,128)(2,1)} %param.11, bf16[768,2048]{1,0:T(8,128)(2,1)} %param.9, f32[2048]{0:T(1024)S(1)} %copy-done.3, f32[768]{0:T(1024)S(1)} %add_rsqrt_fusion), kind=kOutput, calls=%fused_computation.10 | convolution fusion | flops 811794432 | bytes 4598784 | tf_op jit(solution)/shard_map/dot_general | solution.py:49
  43.2 0.4 copy.25
  43.8 1.1 constant_dynamic-slice_fusion.3
  44.9 2.9 %convolution_convert_fusion.1.refs_4_ = bf16[768,128]{1,0:T(8,128)(2,1)S(1)} fusion(bf16[768,2048]{1,0:T(8,128)(2,1)} %param.9, f32[2048]{0:T(1024)S(1)} %copy-done.3, f32[768]{0:T(1024)S(1)} %add_rsqrt_fusion, bf16[2048,1,128]{2,1,0:T(2,128)(2,1)S(1)} %constant_dynamic-slice_fusion.3), kind=kOutput, calls=%fused_computation.11 | convolution fusion | flops 409042944 | bytes 3877888 | tf_op jit(solution)/shard_map/dot_general | solution.py:54
  47.9 1.4 copy.28
  49.3 1.4 copy.29
  50.7 193.6 %shard_map.91 = bf16[768,256]{1,0:T(8,128)(2,1)S(1)} custom-call(s32[10]{0:T(128)S(1)} %pad_add_fusion.bounds_ref, bf16[4,768,64]{2,1,0:T(8,128)(2,1)S(1)} %bitcast.28, bf16[5,1024,128]{2,1,0:T(8,128)(2,1)S(1)} %bitcast.26, s32[5,1,1024]{2,1,0:T(1,128)S(1)} %get-tuple-element.10.refs_1_, bf16[5,1024,128]{2,1,0:T(8,128)(2,1)S(1)} %bitcast.27, ...), custom_call_target="tpu_custom_call" | custom-call | tf_op jit(solution)/shard_map/pallas_call | solution.py:237
  244.4 1.7 collective-permute-done.1
  246.2 1.3 broadcast_in_dim.38
  247.5 5.0 %all-to-all-start.1 = ((bf16[4,384,512]{2,1,0:T(8,128)(2,1)}), bf16[4,384,512]{2,1,0:T(8,128)(2,1)}, u32[]{:S(2)}, u32[]{:S(2)}) async-start(bf16[4,384,512]{2,1,0:T(8,128)(2,1)} %broadcast_in_dim.38), calls=%async_computation.1 | async-start | bytes 3145728 | tf_op jit(solution)/shard_map/all_to_all | solution.py:109
  252.6 3.1 %constant_dynamic-slice_fusion.2 = bf16[2048,512]{1,0:T(8,128)(2,1)} fusion(bf16[2048,2048]{1,0:T(8,128)(2,1)} %param.13, s32[]{:T(128)S(6)} %select_n.109), kind=kLoop, calls=%fused_computation.48 | loop fusion | bytes 4194308 | tf_op jit(solution)/shard_map/dynamic_slice | solution.py:111
  255.6 17.5 %all-to-all-done.1 = bf16[4,384,512]{2,1,0:T(8,128)(2,1)} async-done(((bf16[4,384,512]{2,1,0:T(8,128)(2,1)}), bf16[4,384,512]{2,1,0:T(8,128)(2,1)}, u32[]{:S(2)}, u32[]{:S(2)}) %all-to-all-start.1) | async-done | bytes 1572896 | tf_op jit(solution)/shard_map/all_to_all | solution.py:109
  273.1 3.0 %fusion.3 = bf16[384,512]{1,0:T(8,128)(2,1)S(1)} fusion(bf16[4,384,512]{2,1,0:T(8,128)(2,1)} %all-to-all-done.1, bf16[4,512,512]{2,1,0:T(8,128)(2,1)} %bitcast.30), kind=kOutput, calls=%fused_computation.9 | convolution fusion | flops 805502976 | bytes 4063232 | tf_op jit(solution)/shard_map/zrj,zjn->rn/dot_general | solution.py:113
  276.2 1.4 collective-permute-start.2
  277.6 1.1 collective-permute-done.2
  278.6 0.9 maximum_select_fusion
  (32 shorter events, 1.2 us)
Async XLA Ops:
  0.0 43.8 %copy-start = (bf16[2048,4,128]{2,1,0:T(4,128)(2,1)S(1)}, bf16[2048,4,128]{2,1,0:T(4,128)(2,1)}, u32[]{:S(2)}) copy-start(bf16[2048,4,128]{2,1,0:T(4,128)(2,1)} %param.12) | copy-start | bytes 6291460
  7.7 10.3 %copy-start.1 = (s32[80]{0:T(128)S(1)}, s32[80]{0:T(128)}, u32[]{:S(2)}) copy-start(s32[80]{0:T(128)} %param.17) | copy-start | bytes 964
  7.7 11.5 %copy-start.2 = (s32[80]{0:T(128)S(1)}, s32[80]{0:T(128)}, u32[]{:S(2)}) copy-start(s32[80]{0:T(128)} %param.16) | copy-start | bytes 964
  10.2 29.6 %copy-start.3 = (f32[2048]{0:T(1024)S(1)}, f32[2048]{0:T(1024)}, u32[]{:S(2)}) copy-start(f32[2048]{0:T(1024)} %param.10) | copy-start | bytes 24580
  10.2 26.1 %all-to-all-start = ((bf16[5,16,64,128]{3,2,0,1:T(8,128)(2,1)}), bf16[5,16,64,128]{3,2,0,1:T(8,128)(2,1)}, u32[]{:S(2)}, u32[]{:S(2)}) async-start(bf16[5,16,64,128]{3,2,0,1:T(8,128)(2,1)} %copy.27), calls=%async_computation | async-start | bytes 2621440 | tf_op jit(solution)/shard_map/all_to_all | solution.py:72
  36.3 13.0 %collective-permute-start = (bf16[5,16,64,128]{3,2,0,1:T(8,128)(2,1)}, bf16[5,16,64,128]{3,2,0,1:T(8,128)(2,1)}, u32[]{:S(2)}, u32[]{:S(2)}) collective-permute-start(bf16[5,16,64,128]{3,2,0,1:T(8,128)(2,1)} %all-to-all-done), channel_id=1, source_target_pairs={{0,1},{1,0},{2,3},{3,2},{4,5},{5,4},{6,7},{7,6},{8,9},{9,8},{10,11... | collective-permute-start | bytes 3932168 | tf_op jit(solution)/shard_map/ppermute | solution.py:74
  244.3 1.8 collective-permute-start.1
  247.5 25.6 %all-to-all-start.1 = ((bf16[4,384,512]{2,1,0:T(8,128)(2,1)}), bf16[4,384,512]{2,1,0:T(8,128)(2,1)}, u32[]{:S(2)}, u32[]{:S(2)}) async-start(bf16[4,384,512]{2,1,0:T(8,128)(2,1)} %broadcast_in_dim.38), calls=%async_computation.1 | async-start | bytes 3145728 | tf_op jit(solution)/shard_map/all_to_all | solution.py:109
  276.2 2.5 collective-permute-start.2

commit v6 on v2

--- a/solution.py
+++ b/solution.py
@@ -68,8 +68,8 @@
     head_pages = lax.dynamic_index_in_dim(cache_pages, key_value_head, 1, keepdims=False)
     page_part = head_pages.shape[1] // lax.axis_size("tc")
     head_pages = lax.dynamic_slice_in_dim(head_pages, core_index * page_part, page_part, 1)
-    outgoing = head_pages[held_slot[all_groups].T]
-    incoming = lax.all_to_all(outgoing, "seq", 1, 1, tiled=True)
+    outgoing = head_pages[held_slot[all_groups]]
+    incoming = lax.all_to_all(outgoing, "seq", 0, 0, tiled=True)
     core_count = lax.axis_size("tc")
     partner = lax.ppermute(incoming, "tc", [(0, 1), (1, 0)])
     source_ids = lax.iota(jnp.int32, seq_count)
@@ -86,7 +86,7 @@
     key_parts = []
     for part, half in ((incoming, core_index), (partner, (core_index + 1) % core_count)):
         positions = (page_start + half * page_part + within).reshape(DEVICE_REQUESTS, 1, -1)
-        keys = part.reshape(DEVICE_REQUESTS, -1, 2 * HEAD_SIZE)
+        keys = part.transpose(1, 0, 2, 3).reshape(DEVICE_REQUESTS, -1, 2 * HEAD_SIZE)
         key_parts.append((keys, positions))
     starts = jnp.cumsum(lengths) - lengths
     bounds = jnp.concatenate([starts, starts + lengths]).astype(jnp.int32)
@@ -125,7 +125,7 @@
     return projected
 
 
-BLOCK_ROWS = 128
+BLOCK_ROWS = 64
 
 
 def attend_kernel(window, bounds_ref, q_ref, *refs):

time: 132 us -> 114 us (0.86)
  Pallas kernels: 48.7 us -> 33.3 us
  local copies, waits for them, and re-layouts: 20.1 us -> 17.6 us
    pallas_call x1, Pallas kernels: 48.7 us -> 33.3 us  [attend(): pl.pallas_call(functools.partial(attend_kernel, window), out_shape=jax.Sh...]
    gather x4 -> x3, local copies, waits for them, and re-layouts: 5.66 us -> 3.17 us  [layer(): outgoing = head_pages[held_slot[all_groups]]]
    transpose x0 -> x2, local copies, waits for them, and re-layouts: none -> 1.54 us  [layer(): part.transpose(1, 0, 2, 3).reshape(DEVICE_REQUESTS, -1, 2 * HEAD_SIZE)]
    ppermute x1 -> x0, local copies, waits for them, and re-layouts: 1.43 us -> none  [layer(): partner = lax.ppermute(incoming, 'tc', [(0, 1), (1, 0)])]
  transfers between devices with their start and end apart: 5 -> 5, of which waited for: 4 -> 4; matrix products, arithmetic and copies ran while one was open for 13% -> 15% of each run, Pallas kernels for 0% -> 0%
where the time goes in v6:
time: 114 us; the launch traced here: 113 us
  Pallas kernels  33.3 us (29%)
  waiting for transfers between devices  31.1 us (27%)
  starting transfers between devices  17.7 us (16%)
  local copies, waits for them, and re-layouts  17.6 us (15%)
  matrix products  7.42 us (7%)
  other arithmetic  6.13 us (5%)
    pallas_call x1, Pallas kernels, attend(): pl.pallas_call(functools.partial(attend_kernel, window), out_shape=jax.Sh...  33.3 us
    all_to_all x1, waiting for transfers between devices, layer(): chips_heads = lax.all_to_all(sent, 'tz', 0, 0, tiled=True)  17.5 us
    all_to_all x1, waiting for transfers between devices, layer(): incoming = lax.all_to_all(outgoing, 'seq', 0, 0, tiled=True)  10.8 us
    all_to_all x1, starting transfers between devices, layer(): incoming = lax.all_to_all(outgoing, 'seq', 0, 0, tiled=True)  7.7 us
    all_to_all x1, starting transfers between devices, layer(): chips_heads = lax.all_to_all(sent, 'tz', 0, 0, tiled=True)  5.03 us
    ppermute x1, starting transfers between devices, layer(): partner = lax.ppermute(incoming, 'tc', [(0, 1), (1, 0)])  3.49 us
    dot_general x1, matrix products, layer(): jnp.dot(normed, query_weight, preferred_element_type=jnp.float32)  3.34 us
    gather x3, local copies, waits for them, and re-layouts, layer(): outgoing = head_pages[held_slot[all_groups]]  3.17 us
  transfers between devices with their start and end apart: 5, of which 4 were waited for; matrix products, arithmetic and copies ran while one was open for 15% of the time, Pallas kernels for 0%

profile of v6, /device:TPU:1, one launch (start us, length us, event | category | flops | bytes accessed | tf_op | source)
XLA Modules:
  0.0 113.5 jit_solution(14224224229781495830)
XLA Ops:
  0.0 0.9 add_select_fusion.1
  0.9 0.7 reshape.177
  1.8 0.9 fusion.10
  2.7 1.2 %gather_fusion = s32[80]{0:T(128)S(1)} fusion(s32[16]{0:T(128)S(1)} %fusion.10, s32[1024]{0:T(1024)S(1)} %pad_clamp_fusion.2), kind=kCustom, calls=%fused_computation | custom fusion | bytes 960 | tf_op jit(solution)/shard_map/gather | solution.py:71
  4.0 0.1 reshape.191
  4.1 1.7 %dynamic-slice_bitcast_fusion = bf16[64,64,128]{2,1,0:T(8,128)(2,1)S(1)} fusion(bf16[64,4,128,128]{3,2,1,0:T(8,128)(2,1)} %param.14, s32[]{:T(128)S(6)} %select_n.103, s32[]{:T(128)S(6)} %select_n.105), kind=kLoop, calls=%fused_computation.12 | loop fusion | bytes 2097160 | tf_op jit(solution)/shard_map/dynamic_slice | solution.py:70
  5.8 1.9 %gather_fusion.1 = bf16[80,64,128]{2,1,0:T(8,128)(2,1)} fusion(bf16[64,64,128]{2,1,0:T(8,128)(2,1)S(1)} %dynamic-slice_bitcast_fusion, s32[1024]{0:T(1024)S(1)} %pad_clamp_fusion.1), kind=kCustom, calls=%fused_computation.1 | custom fusion | bytes 2621760 | tf_op jit(solution)/shard_map/gather | solution.py:71
  7.7 7.7 %all-to-all-start = ((bf16[16,5,64,128]{3,2,1,0:T(8,128)(2,1)}), bf16[16,5,64,128]{3,2,1,0:T(8,128)(2,1)S(1)}, u32[]{:S(2)}, u32[]{:S(2)}) async-start(bf16[16,5,64,128]{3,2,1,0:T(8,128)(2,1)} %bitcast.32), calls=%async_computation | async-start | bytes 2621440 | tf_op jit(solution)/shard_map/all_to_all | solution.py:72
  15.5 0.1 select_reduce_fusion
  15.6 0.6 gather_fusion.2
  16.3 0.1 add.179
  16.6 2.7 %fusion = f32[768]{0:T(1024)S(1)} fusion(bf16[768,2048]{1,0:T(8,128)(2,1)} %param.9), kind=kLoop, calls=%fused_computation.5 | loop fusion | flops 4717824 | bytes 3148800 | tf_op jit(solution)/shard_map/reduce_sum | solution.py:25
  19.5 3.3 %convolution_convert_fusion = bf16[768,256]{0,1:T(8,128)(2,1)} fusion(bf16[2048,256]{1,0:T(8,128)(2,1)} %param.11, bf16[768,2048]{1,0:T(8,128)(2,1)S(1)} %copy-done.1, f32[2048]{0:T(1024)S(1)} %copy-done.5, f32[768]{0:T(1024)S(1)} %add_rsqrt_fusion), kind=kOutput, calls=%fused_computation.10 | convolution fusion | flops 811794432 | bytes 4598784 | tf_op jit(solution)/shard_map/dot_general | solution.py:49
  22.8 10.8 %all-to-all-done = bf16[16,5,64,128]{3,2,1,0:T(8,128)(2,1)S(1)} async-done(((bf16[16,5,64,128]{3,2,1,0:T(8,128)(2,1)}), bf16[16,5,64,128]{3,2,1,0:T(8,128)(2,1)S(1)}, u32[]{:S(2)}, u32[]{:S(2)}) %all-to-all-start) | async-done | bytes 1310752 | tf_op jit(solution)/shard_map/all_to_all | solution.py:72
  33.6 3.5 %collective-permute-start = (bf16[16,5,64,128]{3,2,1,0:T(8,128)(2,1)S(1)}, bf16[16,5,64,128]{3,2,1,0:T(8,128)(2,1)}, u32[]{:S(2)}, u32[]{:S(2)}) collective-permute-start(bf16[16,5,64,128]{3,2,1,0:T(8,128)(2,1)S(1)} %all-to-all-done), channel_id=1, source_target_pairs={{0,1},{1,0},{2,3},{3,2},{4,5},{5,4},{6,7},{7,6},{8,9},{9,8},{10,11... | collective-permute-start | bytes 3932168 | tf_op jit(solution)/shard_map/ppermute | solution.py:74
  37.2 0.2 reduce-window.9
  37.4 2.2 %copy.14 = bf16[768,4,64]{2,0,1:T(8,128)(2,1)} copy(bf16[768,4,64]{0,2,1:T(8,128)(2,1)} %bitcast.34) | data formatting | bytes 786432 | tf_op jit(solution)/shard_map/reshape | solution.py:52
  39.7 1.4 %pad_bitcast_fusion.q_ref = bf16[4,768,128]{2,1,0:T(8,128)(2,1)S(1)} fusion(bf16[768,4,64]{2,0,1:T(8,128)(2,1)} %copy.14), kind=kLoop, calls=%fused_computation.17 | loop fusion | bytes 1179648 | tf_op jit(solution)/shard_map/transpose | solution.py:96
  41.2 1.1 %constant_dynamic-slice_fusion.3 = bf16[2048,1,128]{2,1,0:T(2,128)(2,1)S(1)} fusion(bf16[2048,4,128]{2,1,0:T(4,128)(2,1)S(1)} %copy-done, s32[]{:T(128)S(6)} %select_n.102), kind=kLoop, calls=%fused_computation.50 | loop fusion | bytes 1048580 | tf_op jit(solution)/shard_map/jit(dynamic_index_in_dim)/dynamic_slice | solution.py:53
  42.4 1.0 convolution_convert_fusion.1.refs_4_
  43.4 0.1 copy.15
  43.5 1.4 %copy.16 = bf16[5,16,64,128]{3,2,1,0:T(8,128)(2,1)S(1)} copy(bf16[5,16,64,128]{3,2,0,1:T(8,128)(2,1)} %bitcast.8) | data formatting | bytes 2621440 | tf_op jit(solution)/shard_map/transpose | solution.py:89
  45.0 33.3 %shard_map.91 = bf16[768,256]{1,0:T(8,128)(2,1)S(1)} custom-call(s32[10]{0:T(128)S(1)} %pad_add_fusion.bounds_ref, bf16[4,768,128]{2,1,0:T(8,128)(2,1)S(1)} %pad_bitcast_fusion.q_ref, bf16[5,1024,128]{2,1,0:T(8,128)(2,1)S(1)} %bitcast.29, s32[5,1,1024]{2,1,0:T(1,128)S(1)} %get-tuple-element.10.refs_1_, bf16[5,1024,128]{2,1,0:T(8,128)(2,1)S(1)} %bitcast.30, ...), custom_call_target="tpu_custom_call" | custom-call | tf_op jit(solution)/shard_map/pallas_call | solution.py:202
  78.4 1.7 %collective-permute-done.1 = bf16[768,256]{1,0:T(8,128)(2,1)S(1)} collective-permute-done((bf16[768,256]{1,0:T(8,128)(2,1)S(1)}, bf16[768,256]{1,0:T(8,128)(2,1)S(1)}, u32[]{:S(2)}, u32[]{:S(2)}) %collective-permute-start.1) | collective-permute-done | bytes 393248 | tf_op jit(solution)/shard_map/ppermute | solution.py:101
  80.2 1.3 %broadcast_in_dim.21 = bf16[4,384,512]{2,1,0:T(8,128)(2,1)} broadcast(bf16[384,512]{1,0:T(8,128)(2,1)S(1)} %fusion.7), dimensions={1,2} | broadcast | bytes 1966080 | tf_op jit(solution)/shard_map/broadcast_in_dim | solution.py:110
  81.4 5.0 %all-to-all-start.1 = ((bf16[4,384,512]{2,1,0:T(8,128)(2,1)}), bf16[4,384,512]{2,1,0:T(8,128)(2,1)}, u32[]{:S(2)}, u32[]{:S(2)}) async-start(bf16[4,384,512]{2,1,0:T(8,128)(2,1)} %broadcast_in_dim.21), calls=%async_computation.1 | async-start | bytes 3145728 | tf_op jit(solution)/shard_map/all_to_all | solution.py:111
  86.5 3.1 %constant_dynamic-slice_fusion.2 = bf16[2048,512]{1,0:T(8,128)(2,1)} fusion(bf16[2048,2048]{1,0:T(8,128)(2,1)} %param.13, s32[]{:T(128)S(6)} %select_n.116), kind=kLoop, calls=%fused_computation.49 | loop fusion | bytes 4194308 | tf_op jit(solution)/shard_map/dynamic_slice | solution.py:113
  89.5 17.5 %all-to-all-done.1 = bf16[4,384,512]{2,1,0:T(8,128)(2,1)} async-done(((bf16[4,384,512]{2,1,0:T(8,128)(2,1)}), bf16[4,384,512]{2,1,0:T(8,128)(2,1)}, u32[]{:S(2)}, u32[]{:S(2)}) %all-to-all-start.1) | async-done | bytes 1572896 | tf_op jit(solution)/shard_map/all_to_all | solution.py:111
  107.0 3.0 %fusion.3 = bf16[384,512]{1,0:T(8,128)(2,1)S(1)} fusion(bf16[4,384,512]{2,1,0:T(8,128)(2,1)} %all-to-all-done.1, bf16[4,512,512]{2,1,0:T(8,128)(2,1)} %bitcast.33), kind=kOutput, calls=%fused_computation.9 | convolution fusion | flops 805502976 | bytes 4063232 | tf_op jit(solution)/shard_map/zrj,zjn->rn/dot_general | solution.py:115
  110.1 1.4 %collective-permute-start.2 = (bf16[384,256]{1,0:T(8,128)(2,1)S(1)}, bf16[384,256]{1,0:T(8,128)(2,1)S(1)}, u32[]{:S(2)}, u32[]{:S(2)}) collective-permute-start(bf16[384,256]{1,0:T(8,128)(2,1)S(1)} %get-tuple-element.8), channel_id=1, source_target_pairs={{0,1},{1,0},{2,3},{3,2},{4,5},{5,4},{6,7},{7,6},{8,9},{9,8},{10,11... | collective-permute-start | bytes 589832 | tf_op jit(solution)/shard_map/ppermute | solution.py:121
  111.5 1.1 collective-permute-done.2
  112.6 0.9 maximum_select_fusion
  (35 shorter events, 1.2 us)
Async XLA Ops:
  0.0 41.2 %copy-start = (bf16[2048,4,128]{2,1,0:T(4,128)(2,1)S(1)}, bf16[2048,4,128]{2,1,0:T(4,128)(2,1)}, u32[]{:S(2)}) copy-start(bf16[2048,4,128]{2,1,0:T(4,128)(2,1)} %param.12) | copy-start | bytes 6291460
  5.8 9.6 %copy-start.3 = (s32[80]{0:T(128)S(1)}, s32[80]{0:T(128)}, u32[]{:S(2)}) copy-start(s32[80]{0:T(128)} %param.17) | copy-start | bytes 964
  7.7 11.7 %copy-start.5 = (f32[2048]{0:T(1024)S(1)}, f32[2048]{0:T(1024)}, u32[]{:S(2)}) copy-start(f32[2048]{0:T(1024)} %param.10) | copy-start | bytes 24580
  7.7 26.0 %all-to-all-start = ((bf16[16,5,64,128]{3,2,1,0:T(8,128)(2,1)}), bf16[16,5,64,128]{3,2,1,0:T(8,128)(2,1)S(1)}, u32[]{:S(2)}, u32[]{:S(2)}) async-start(bf16[16,5,64,128]{3,2,1,0:T(8,128)(2,1)} %bitcast.32), calls=%async_computation | async-start | bytes 2621440 | tf_op jit(solution)/shard_map/all_to_all | solution.py:72
  16.6 2.8 %copy-start.1 = (bf16[768,2048]{1,0:T(8,128)(2,1)S(1)}, bf16[768,2048]{1,0:T(8,128)(2,1)}, u32[]{:S(2)}) copy-start(bf16[768,2048]{1,0:T(8,128)(2,1)} %param.9) | copy-start | bytes 9437188
  19.5 17.7 %copy-start.4 = (s32[80]{0:T(128)S(1)}, s32[80]{0:T(128)}, u32[]{:S(2)}) copy-start(s32[80]{0:T(128)} %param.16) | copy-start | bytes 964
  33.6 9.9 %collective-permute-start = (bf16[16,5,64,128]{3,2,1,0:T(8,128)(2,1)S(1)}, bf16[16,5,64,128]{3,2,1,0:T(8,128)(2,1)}, u32[]{:S(2)}, u32[]{:S(2)}) collective-permute-start(bf16[16,5,64,128]{3,2,1,0:T(8,128)(2,1)S(1)} %all-to-all-done), channel_id=1, source_target_pairs={{0,1},{1,0},{2,3},{3,2},{4,5},{5,4},{6,7},{7,6},{8,9},{9,8},{10,11... | collective-permute-start | bytes 3932168 | tf_op jit(solution)/shard_map/ppermute | solution.py:74
  39.6 2.8 %copy-start.2 = (bf16[768,2048]{1,0:T(8,128)(2,1)S(1)}, bf16[768,2048]{1,0:T(8,128)(2,1)}, u32[]{:S(2)}) copy-start(bf16[768,2048]{1,0:T(8,128)(2,1)} %param.9) | copy-start | bytes 9437188
  78.3 1.8 %collective-permute-start.1 = (bf16[768,256]{1,0:T(8,128)(2,1)S(1)}, bf16[768,256]{1,0:T(8,128)(2,1)S(1)}, u32[]{:S(2)}, u32[]{:S(2)}) collective-permute-start(bf16[768,256]{1,0:T(8,128)(2,1)S(1)} %shard_map.91), channel_id=1, source_target_pairs={{0,1},{1,0},{2,3},{3,2},{4,5},{5,4},{6,7},{7,6},{8,9},{9,8},{10,11... | collective-permute-start | bytes 1179656 | tf_op jit(solution)/shard_map/ppermute | solution.py:101
  81.4 25.6 %all-to-all-start.1 = ((bf16[4,384,512]{2,1,0:T(8,128)(2,1)}), bf16[4,384,512]{2,1,0:T(8,128)(2,1)}, u32[]{:S(2)}, u32[]{:S(2)}) async-start(bf16[4,384,512]{2,1,0:T(8,128)(2,1)} %broadcast_in_dim.21), calls=%async_computation.1 | async-start | bytes 3145728 | tf_op jit(solution)/shard_map/all_to_all | solution.py:111
  110.1 2.5 %collective-permute-start.2 = (bf16[384,256]{1,0:T(8,128)(2,1)S(1)}, bf16[384,256]{1,0:T(8,128)(2,1)S(1)}, u32[]{:S(2)}, u32[]{:S(2)}) collective-permute-start(bf16[384,256]{1,0:T(8,128)(2,1)S(1)} %get-tuple-element.8), channel_id=1, source_target_pairs={{0,1},{1,0},{2,3},{3,2},{4,5},{5,4},{6,7},{7,6},{8,9},{9,8},{10,11... | collective-permute-start | bytes 589832 | tf_op jit(solution)/shard_map/ppermute | solution.py:121

commit v7 on v6

--- a/solution.py
+++ b/solution.py
@@ -65,10 +65,10 @@
     local_slot = tail_ids % pages_here
     held_slot = jnp.sum(jnp.where(holder == seq_index, local_slot, 0), axis=1)
     all_groups = request_groups.reshape(seq_count, DEVICE_REQUESTS)
-    head_pages = lax.dynamic_index_in_dim(cache_pages, key_value_head, 1, keepdims=False)
-    page_part = head_pages.shape[1] // lax.axis_size("tc")
-    head_pages = lax.dynamic_slice_in_dim(head_pages, core_index * page_part, page_part, 1)
-    outgoing = head_pages[held_slot[all_groups]]
+    page_part = cache_pages.shape[2] // lax.axis_size("tc")
+    outgoing = lax.dynamic_slice_in_dim(
+        cache_pages[held_slot[all_groups], key_value_head], core_index * page_part, page_part, 2
+    )
     incoming = lax.all_to_all(outgoing, "seq", 0, 0, tiled=True)
     core_count = lax.axis_size("tc")
     partner = lax.ppermute(incoming, "tc", [(0, 1), (1, 0)])

time: 114 us -> 119 us (1.044)
  local copies, waits for them, and re-layouts: 17.6 us -> 22.8 us
    gather x3, local copies, waits for them, and re-layouts: 3.17 us -> 7.61 us  [the longest x1 6.3 us: layer(): cache_pages[held_slot[all_groups], key_value_head]]
  transfers between devices with their start and end apart: 5 -> 5, of which waited for: 4 -> 4; matrix products, arithmetic and copies ran while one was open for 15% -> 14% of each run, Pallas kernels for 0% -> 0%
where the time goes in v7:
time: 119 us
  Pallas kernels  33.3 us (28%)
  waiting for transfers between devices  31.1 us (26%)
  local copies, waits for them, and re-layouts  22.8 us (19%)
  starting transfers between devices  17.7 us (15%)
  matrix products  7.42 us (6%)
  other arithmetic  6.13 us (5%)
    pallas_call x1, Pallas kernels, attend(): pl.pallas_call(functools.partial(attend_kernel, window), out_shape=jax.Sh...  33.3 us
    all_to_all x1, waiting for transfers between devices, layer(): chips_heads = lax.all_to_all(sent, 'tz', 0, 0, tiled=True)  17.5 us
    all_to_all x1, waiting for transfers between devices, layer(): incoming = lax.all_to_all(outgoing, 'seq', 0, 0, tiled=True)  10.8 us
    all_to_all x1, starting transfers between devices, layer(): incoming = lax.all_to_all(outgoing, 'seq', 0, 0, tiled=True)  7.7 us
    gather x1, local copies, waits for them, and re-layouts, layer(): cache_pages[held_slot[all_groups], key_value_head]  6.3 us
    all_to_all x1, starting transfers between devices, layer(): chips_heads = lax.all_to_all(sent, 'tz', 0, 0, tiled=True)  5.02 us
    ppermute x1, starting transfers between devices, layer(): partner = lax.ppermute(incoming, 'tc', [(0, 1), (1, 0)])  3.49 us
    dot_general x1, matrix products, layer(): jnp.dot(normed, query_weight, preferred_element_type=jnp.float32)  3.33 us
  transfers between devices with their start and end apart: 5, of which 4 were waited for; matrix products, arithmetic and copies ran while one was open for 14% of the time, Pallas kernels for 0%

profile of v7, /device:TPU:1, one launch (start us, length us, event | category | flops | bytes accessed | tf_op | source)
XLA Modules:
  0.0 118.7 jit_solution(10103177962341262222)
XLA Ops:
  0.0 0.9 add_select_fusion.1
  0.9 0.7 reshape.176
  1.8 0.9 fusion.10
  2.7 1.2 %gather_fusion = s32[80]{0:T(128)S(1)} fusion(s32[16]{0:T(128)S(1)} %fusion.10, s32[1024]{0:T(1024)S(1)} %pad_clamp_fusion.1), kind=kCustom, calls=%fused_computation | custom fusion | bytes 960 | tf_op jit(solution)/shard_map/gather | solution.py:70
  4.1 6.3 %gather_fusion.1 = bf16[80,128,128]{2,1,0:T(8,128)(2,1)} fusion(bf16[64,4,128,128]{3,2,1,0:T(8,128)(2,1)} %param.14, s32[80]{0:T(128)S(1)} %reshape.188), kind=kCustom, calls=%fused_computation.1 | custom fusion | bytes 5243520 | tf_op jit(solution)/shard_map/gather | solution.py:70
  10.4 2.5 %constant_dynamic-slice_fusion.4 = bf16[16,5,64,128]{3,2,1,0:T(8,128)(2,1)} fusion(bf16[16,5,128,128]{3,2,1,0:T(8,128)(2,1)} %bitcast.29, s32[]{:T(128)S(6)} %select_n.103), kind=kLoop, calls=%fused_computation.52 | loop fusion | bytes 2621444 | tf_op jit(solution)/shard_map/dynamic_slice | solution.py:69
  12.9 7.7 %all-to-all-start = ((bf16[16,5,64,128]{3,2,1,0:T(8,128)(2,1)}), bf16[16,5,64,128]{3,2,1,0:T(8,128)(2,1)S(1)}, u32[]{:S(2)}, u32[]{:S(2)}) async-start(bf16[16,5,64,128]{3,2,1,0:T(8,128)(2,1)} %constant_dynamic-slice_fusion.4), calls=%async_computation | async-start | bytes 2621440 | tf_op jit(solution)/shard_map/all_to_all | solution.py:72
  20.7 0.1 select_reduce_fusion
  20.9 0.6 gather_fusion.2
  21.5 0.1 add.176
  21.9 2.7 %fusion = f32[768]{0:T(1024)S(1)} fusion(bf16[768,2048]{1,0:T(8,128)(2,1)} %param.9), kind=kLoop, calls=%fused_computation.5 | loop fusion | flops 4717824 | bytes 3148800 | tf_op jit(solution)/shard_map/reduce_sum | solution.py:25
  24.7 3.3 %convolution_convert_fusion = bf16[768,256]{0,1:T(8,128)(2,1)} fusion(bf16[2048,256]{1,0:T(8,128)(2,1)} %param.11, bf16[768,2048]{1,0:T(8,128)(2,1)S(1)} %copy-done.1, f32[2048]{0:T(1024)S(1)} %copy-done.5, f32[768]{0:T(1024)S(1)} %add_rsqrt_fusion), kind=kOutput, calls=%fused_computation.10 | convolution fusion | flops 811794432 | bytes 4598784 | tf_op jit(solution)/shard_map/dot_general | solution.py:49
  28.0 10.8 %all-to-all-done = bf16[16,5,64,128]{3,2,1,0:T(8,128)(2,1)S(1)} async-done(((bf16[16,5,64,128]{3,2,1,0:T(8,128)(2,1)}), bf16[16,5,64,128]{3,2,1,0:T(8,128)(2,1)S(1)}, u32[]{:S(2)}, u32[]{:S(2)}) %all-to-all-start) | async-done | bytes 1310752 | tf_op jit(solution)/shard_map/all_to_all | solution.py:72
  38.9 3.5 %collective-permute-start = (bf16[16,5,64,128]{3,2,1,0:T(8,128)(2,1)S(1)}, bf16[16,5,64,128]{3,2,1,0:T(8,128)(2,1)}, u32[]{:S(2)}, u32[]{:S(2)}) collective-permute-start(bf16[16,5,64,128]{3,2,1,0:T(8,128)(2,1)S(1)} %all-to-all-done), channel_id=1, source_target_pairs={{0,1},{1,0},{2,3},{3,2},{4,5},{5,4},{6,7},{7,6},{8,9},{9,8},{10,11... | collective-permute-start | bytes 3932168 | tf_op jit(solution)/shard_map/ppermute | solution.py:74
  42.4 0.2 reduce-window.9
  42.6 2.2 %copy.18 = bf16[768,4,64]{2,0,1:T(8,128)(2,1)} copy(bf16[768,4,64]{0,2,1:T(8,128)(2,1)} %bitcast.32) | data formatting | bytes 786432 | tf_op jit(solution)/shard_map/reshape | solution.py:52
  45.0 1.4 %pad_bitcast_fusion.q_ref = bf16[4,768,128]{2,1,0:T(8,128)(2,1)S(1)} fusion(bf16[768,4,64]{2,0,1:T(8,128)(2,1)} %copy.18), kind=kLoop, calls=%fused_computation.16 | loop fusion | bytes 1179648 | tf_op jit(solution)/shard_map/transpose | solution.py:96
  46.4 1.1 constant_dynamic-slice_fusion.3
  47.6 1.0 convolution_convert_fusion.1.refs_4_
  48.7 0.1 copy.19
  48.8 1.4 %copy.20 = bf16[5,16,64,128]{3,2,1,0:T(8,128)(2,1)S(1)} copy(bf16[5,16,64,128]{3,2,0,1:T(8,128)(2,1)} %bitcast.7) | data formatting | bytes 2621440 | tf_op jit(solution)/shard_map/transpose | solution.py:89
  50.2 33.3 %shard_map.91 = bf16[768,256]{1,0:T(8,128)(2,1)S(1)} custom-call(s32[10]{0:T(128)S(1)} %pad_add_fusion.bounds_ref, bf16[4,768,128]{2,1,0:T(8,128)(2,1)S(1)} %pad_bitcast_fusion.q_ref, bf16[5,1024,128]{2,1,0:T(8,128)(2,1)S(1)} %bitcast.27, s32[5,1,1024]{2,1,0:T(1,128)S(1)} %get-tuple-element.10.refs_1_, bf16[5,1024,128]{2,1,0:T(8,128)(2,1)S(1)} %bitcast.28, ...), custom_call_target="tpu_custom_call" | custom-call | tf_op jit(solution)/shard_map/pallas_call | solution.py:202
  83.6 1.7 %collective-permute-done.1 = bf16[768,256]{1,0:T(8,128)(2,1)S(1)} collective-permute-done((bf16[768,256]{1,0:T(8,128)(2,1)S(1)}, bf16[768,256]{1,0:T(8,128)(2,1)S(1)}, u32[]{:S(2)}, u32[]{:S(2)}) %collective-permute-start.1) | collective-permute-done | bytes 393248 | tf_op jit(solution)/shard_map/ppermute | solution.py:101
  85.3 0.1 fusion.7
  85.4 1.3 %broadcast_in_dim.21 = bf16[4,384,512]{2,1,0:T(8,128)(2,1)} broadcast(bf16[384,512]{1,0:T(8,128)(2,1)S(1)} %fusion.7), dimensions={1,2} | broadcast | bytes 1966080 | tf_op jit(solution)/shard_map/broadcast_in_dim | solution.py:110
  86.7 5.0 %all-to-all-start.1 = ((bf16[4,384,512]{2,1,0:T(8,128)(2,1)}), bf16[4,384,512]{2,1,0:T(8,128)(2,1)}, u32[]{:S(2)}, u32[]{:S(2)}) async-start(bf16[4,384,512]{2,1,0:T(8,128)(2,1)} %broadcast_in_dim.21), calls=%async_computation.1 | async-start | bytes 3145728 | tf_op jit(solution)/shard_map/all_to_all | solution.py:111
  91.7 3.1 %constant_dynamic-slice_fusion.2 = bf16[2048,512]{1,0:T(8,128)(2,1)} fusion(bf16[2048,2048]{1,0:T(8,128)(2,1)} %param.13, s32[]{:T(128)S(6)} %select_n.109), kind=kLoop, calls=%fused_computation.50 | loop fusion | bytes 4194308 | tf_op jit(solution)/shard_map/dynamic_slice | solution.py:113
  94.8 17.5 %all-to-all-done.1 = bf16[4,384,512]{2,1,0:T(8,128)(2,1)} async-done(((bf16[4,384,512]{2,1,0:T(8,128)(2,1)}), bf16[4,384,512]{2,1,0:T(8,128)(2,1)}, u32[]{:S(2)}, u32[]{:S(2)}) %all-to-all-start.1) | async-done | bytes 1572896 | tf_op jit(solution)/shard_map/all_to_all | solution.py:111
  112.2 3.0 %fusion.3 = bf16[384,512]{1,0:T(8,128)(2,1)S(1)} fusion(bf16[4,384,512]{2,1,0:T(8,128)(2,1)} %all-to-all-done.1, bf16[4,512,512]{2,1,0:T(8,128)(2,1)} %bitcast.31), kind=kOutput, calls=%fused_computation.9 | convolution fusion | flops 805502976 | bytes 4063232 | tf_op jit(solution)/shard_map/zrj,zjn->rn/dot_general | solution.py:115
  115.3 1.4 %collective-permute-start.2 = (bf16[384,256]{1,0:T(8,128)(2,1)S(1)}, bf16[384,256]{1,0:T(8,128)(2,1)S(1)}, u32[]{:S(2)}, u32[]{:S(2)}) collective-permute-start(bf16[384,256]{1,0:T(8,128)(2,1)S(1)} %get-tuple-element.8), channel_id=1, source_target_pairs={{0,1},{1,0},{2,3},{3,2},{4,5},{5,4},{6,7},{7,6},{8,9},{9,8},{10,11... | collective-permute-start | bytes 589832 | tf_op jit(solution)/shard_map/ppermute | solution.py:121
  116.7 1.1 collective-permute-done.2
  117.8 0.9 maximum_select_fusion
  (34 shorter events, 1.2 us)
Async XLA Ops:
  0.0 46.4 %copy-start = (bf16[2048,4,128]{2,1,0:T(4,128)(2,1)S(1)}, bf16[2048,4,128]{2,1,0:T(4,128)(2,1)}, u32[]{:S(2)}) copy-start(bf16[2048,4,128]{2,1,0:T(4,128)(2,1)} %param.12) | copy-start | bytes 6291460
  10.4 10.2 %copy-start.3 = (s32[80]{0:T(128)S(1)}, s32[80]{0:T(128)}, u32[]{:S(2)}) copy-start(s32[80]{0:T(128)} %param.17) | copy-start | bytes 964
  12.9 11.7 %copy-start.5 = (f32[2048]{0:T(1024)S(1)}, f32[2048]{0:T(1024)}, u32[]{:S(2)}) copy-start(f32[2048]{0:T(1024)} %param.10) | copy-start | bytes 24580
  12.9 26.0 %all-to-all-start = ((bf16[16,5,64,128]{3,2,1,0:T(8,128)(2,1)}), bf16[16,5,64,128]{3,2,1,0:T(8,128)(2,1)S(1)}, u32[]{:S(2)}, u32[]{:S(2)}) async-start(bf16[16,5,64,128]{3,2,1,0:T(8,128)(2,1)} %constant_dynamic-slice_fusion.4), calls=%async_computation | async-start | bytes 2621440 | tf_op jit(solution)/shard_map/all_to_all | solution.py:72
  21.9 2.8 %copy-start.1 = (bf16[768,2048]{1,0:T(8,128)(2,1)S(1)}, bf16[768,2048]{1,0:T(8,128)(2,1)}, u32[]{:S(2)}) copy-start(bf16[768,2048]{1,0:T(8,128)(2,1)} %param.9) | copy-start | bytes 9437188
  24.7 17.7 %copy-start.4 = (s32[80]{0:T(128)S(1)}, s32[80]{0:T(128)}, u32[]{:S(2)}) copy-start(s32[80]{0:T(128)} %param.16) | copy-start | bytes 964
  38.9 9.9 %collective-permute-start = (bf16[16,5,64,128]{3,2,1,0:T(8,128)(2,1)S(1)}, bf16[16,5,64,128]{3,2,1,0:T(8,128)(2,1)}, u32[]{:S(2)}, u32[]{:S(2)}) collective-permute-start(bf16[16,5,64,128]{3,2,1,0:T(8,128)(2,1)S(1)} %all-to-all-done), channel_id=1, source_target_pairs={{0,1},{1,0},{2,3},{3,2},{4,5},{5,4},{6,7},{7,6},{8,9},{9,8},{10,11... | collective-permute-start | bytes 3932168 | tf_op jit(solution)/shard_map/ppermute | solution.py:74
  44.8 2.8 %copy-start.2 = (bf16[768,2048]{1,0:T(8,128)(2,1)S(1)}, bf16[768,2048]{1,0:T(8,128)(2,1)}, u32[]{:S(2)}) copy-start(bf16[768,2048]{1,0:T(8,128)(2,1)} %param.9) | copy-start | bytes 9437188
  83.5 1.8 %collective-permute-start.1 = (bf16[768,256]{1,0:T(8,128)(2,1)S(1)}, bf16[768,256]{1,0:T(8,128)(2,1)S(1)}, u32[]{:S(2)}, u32[]{:S(2)}) collective-permute-start(bf16[768,256]{1,0:T(8,128)(2,1)S(1)} %shard_map.91), channel_id=1, source_target_pairs={{0,1},{1,0},{2,3},{3,2},{4,5},{5,4},{6,7},{7,6},{8,9},{9,8},{10,11... | collective-permute-start | bytes 1179656 | tf_op jit(solution)/shard_map/ppermute | solution.py:101
  86.7 25.6 %all-to-all-start.1 = ((bf16[4,384,512]{2,1,0:T(8,128)(2,1)}), bf16[4,384,512]{2,1,0:T(8,128)(2,1)}, u32[]{:S(2)}, u32[]{:S(2)}) async-start(bf16[4,384,512]{2,1,0:T(8,128)(2,1)} %broadcast_in_dim.21), calls=%async_computation.1 | async-start | bytes 3145728 | tf_op jit(solution)/shard_map/all_to_all | solution.py:111
  115.3 2.5 %collective-permute-start.2 = (bf16[384,256]{1,0:T(8,128)(2,1)S(1)}, bf16[384,256]{1,0:T(8,128)(2,1)S(1)}, u32[]{:S(2)}, u32[]{:S(2)}) collective-permute-start(bf16[384,256]{1,0:T(8,128)(2,1)S(1)} %get-tuple-element.8), channel_id=1, source_target_pairs={{0,1},{1,0},{2,3},{3,2},{4,5},{5,4},{6,7},{7,6},{8,9},{9,8},{10,11... | collective-permute-start | bytes 589832 | tf_op jit(solution)/shard_map/ppermute | solution.py:121

commit v8 on v6

--- a/solution.py
+++ b/solution.py
@@ -98,15 +98,18 @@
     swap = [(0, 1), (1, 0)]
     z_count = lax.axis_size("tz")
     z_index = lax.axis_index("tz")
-    partner_heads = lax.ppermute(attended, "tc", swap)
     first_core = core_index == 0
-    chip_heads = jnp.where(
+    half_rows = row_count // core_count
+    own_rows = lax.dynamic_slice_in_dim(attended, core_index * half_rows, half_rows, 0)
+    partner_rows = lax.dynamic_slice_in_dim(
+        attended, (1 - core_index) * half_rows, half_rows, 0
+    )
+    partner_heads = lax.ppermute(partner_rows, "tc", swap)
+    my_half = jnp.where(
         first_core,
-        jnp.concatenate([attended, partner_heads], axis=1),
-        jnp.concatenate([partner_heads, attended], axis=1),
-    )
-    half_rows = row_count // core_count
-    my_half = lax.dynamic_slice_in_dim(chip_heads, core_index * half_rows, half_rows, 0)
+        jnp.concatenate([own_rows, partner_heads], axis=1),
+        jnp.concatenate([partner_heads, own_rows], axis=1),
+    )
     sent = jnp.broadcast_to(my_half[None], (z_count,) + my_half.shape)
     chips_heads = lax.all_to_all(sent, "tz", 0, 0, tiled=True)
     chip_width = out_weight.shape[1] // z_count

time: 114 us -> 114 us (level)
  no operation moved by 1% of the time
where the time goes in v8:
time: 114 us; the launch traced here: 113 us
  Pallas kernels  33.3 us (29%)
  waiting for transfers between devices  30.8 us (27%)
  starting transfers between devices  17.7 us (16%)
  local copies, waits for them, and re-layouts  17.6 us (15%)
  matrix products  7.41 us (6%)
  other arithmetic  6.13 us (5%)
    pallas_call x1, Pallas kernels, attend(): pl.pallas_call(functools.partial(attend_kernel, window), out_shape=jax.Sh...  33.3 us
    all_to_all x1, waiting for transfers between devices, layer(): chips_heads = lax.all_to_all(sent, 'tz', 0, 0, tiled=True)  17.4 us
    all_to_all x1, waiting for transfers between devices, layer(): incoming = lax.all_to_all(outgoing, 'seq', 0, 0, tiled=True)  10.8 us
    all_to_all x1, starting transfers between devices, layer(): incoming = lax.all_to_all(outgoing, 'seq', 0, 0, tiled=True)  7.7 us
    all_to_all x1, starting transfers between devices, layer(): chips_heads = lax.all_to_all(sent, 'tz', 0, 0, tiled=True)  5.03 us
    ppermute x1, starting transfers between devices, layer(): partner = lax.ppermute(incoming, 'tc', [(0, 1), (1, 0)])  3.49 us
    dot_general x1, matrix products, layer(): jnp.dot(normed, query_weight, preferred_element_type=jnp.float32)  3.33 us
    gather x3, local copies, waits for them, and re-layouts, layer(): outgoing = head_pages[held_slot[all_groups]]  3.18 us
  transfers between devices with their start and end apart: 5, of which 4 were waited for; matrix products, arithmetic and copies ran while one was open for 15% of the time, Pallas kernels for 0%

profile of v8, /device:TPU:1, one launch (start us, length us, event | category | flops | bytes accessed | tf_op | source)
XLA Modules:
  0.0 113.2 jit_solution(9755104193231923702)
XLA Ops:
  0.0 0.9 add_select_fusion.1
  0.9 0.7 reshape.205
  1.8 0.9 fusion.7
  2.7 1.2 %gather_fusion = s32[80]{0:T(128)S(1)} fusion(s32[16]{0:T(128)S(1)} %fusion.7, s32[1024]{0:T(1024)S(1)} %pad_clamp_fusion.2), kind=kCustom, calls=%fused_computation | custom fusion | bytes 960 | tf_op jit(solution)/shard_map/gather | solution.py:71
  4.0 0.1 reshape.219
  4.1 1.7 %dynamic-slice_bitcast_fusion = bf16[64,64,128]{2,1,0:T(8,128)(2,1)S(1)} fusion(bf16[64,4,128,128]{3,2,1,0:T(8,128)(2,1)} %param.14, s32[]{:T(128)S(6)} %select_n.110, s32[]{:T(128)S(6)} %select_n.112), kind=kLoop, calls=%fused_computation.12 | loop fusion | bytes 2097160 | tf_op jit(solution)/shard_map/dynamic_slice | solution.py:70
  5.8 1.9 %gather_fusion.1 = bf16[80,64,128]{2,1,0:T(8,128)(2,1)} fusion(bf16[64,64,128]{2,1,0:T(8,128)(2,1)S(1)} %dynamic-slice_bitcast_fusion, s32[1024]{0:T(1024)S(1)} %pad_clamp_fusion.1), kind=kCustom, calls=%fused_computation.1 | custom fusion | bytes 2621760 | tf_op jit(solution)/shard_map/gather | solution.py:71
  7.7 7.7 %all-to-all-start = ((bf16[16,5,64,128]{3,2,1,0:T(8,128)(2,1)}), bf16[16,5,64,128]{3,2,1,0:T(8,128)(2,1)S(1)}, u32[]{:S(2)}, u32[]{:S(2)}) async-start(bf16[16,5,64,128]{3,2,1,0:T(8,128)(2,1)} %bitcast.32), calls=%async_computation | async-start | bytes 2621440 | tf_op jit(solution)/shard_map/all_to_all | solution.py:72
  15.5 0.1 select_reduce_fusion
  15.6 0.6 gather_fusion.2
  16.4 0.1 add.192
  16.6 2.7 %fusion = f32[768]{0:T(1024)S(1)} fusion(bf16[768,2048]{1,0:T(8,128)(2,1)} %param.9), kind=kLoop, calls=%fused_computation.5 | loop fusion | flops 4717824 | bytes 3148800 | tf_op jit(solution)/shard_map/reduce_sum | solution.py:25
  19.5 3.3 %convolution_convert_fusion = bf16[768,256]{0,1:T(8,128)(2,1)} fusion(bf16[2048,256]{1,0:T(8,128)(2,1)} %param.11, bf16[768,2048]{1,0:T(8,128)(2,1)S(1)} %copy-done.1, f32[2048]{0:T(1024)S(1)} %copy-done.5, f32[768]{0:T(1024)S(1)} %add_rsqrt_fusion), kind=kOutput, calls=%fused_computation.10 | convolution fusion | flops 811794432 | bytes 4598784 | tf_op jit(solution)/shard_map/dot_general | solution.py:49
  22.8 10.8 %all-to-all-done = bf16[16,5,64,128]{3,2,1,0:T(8,128)(2,1)S(1)} async-done(((bf16[16,5,64,128]{3,2,1,0:T(8,128)(2,1)}), bf16[16,5,64,128]{3,2,1,0:T(8,128)(2,1)S(1)}, u32[]{:S(2)}, u32[]{:S(2)}) %all-to-all-start) | async-done | bytes 1310752 | tf_op jit(solution)/shard_map/all_to_all | solution.py:72
  33.6 3.5 %collective-permute-start = (bf16[16,5,64,128]{3,2,1,0:T(8,128)(2,1)S(1)}, bf16[16,5,64,128]{3,2,1,0:T(8,128)(2,1)}, u32[]{:S(2)}, u32[]{:S(2)}) collective-permute-start(bf16[16,5,64,128]{3,2,1,0:T(8,128)(2,1)S(1)} %all-to-all-done), channel_id=1, source_target_pairs={{0,1},{1,0},{2,3},{3,2},{4,5},{5,4},{6,7},{7,6},{8,9},{9,8},{10,11... | collective-permute-start | bytes 3932168 | tf_op jit(solution)/shard_map/ppermute | solution.py:74
  37.2 0.2 reduce-window.9
  37.4 2.2 %copy.14 = bf16[768,4,64]{2,0,1:T(8,128)(2,1)} copy(bf16[768,4,64]{0,2,1:T(8,128)(2,1)} %bitcast.34) | data formatting | bytes 786432 | tf_op jit(solution)/shard_map/reshape | solution.py:52
  39.7 1.4 %pad_bitcast_fusion.q_ref = bf16[4,768,128]{2,1,0:T(8,128)(2,1)S(1)} fusion(bf16[768,4,64]{2,0,1:T(8,128)(2,1)} %copy.14), kind=kLoop, calls=%fused_computation.13 | loop fusion | bytes 1179648 | tf_op jit(solution)/shard_map/transpose | solution.py:96
  41.2 1.1 %constant_dynamic-slice_fusion.5 = bf16[2048,1,128]{2,1,0:T(2,128)(2,1)S(1)} fusion(bf16[2048,4,128]{2,1,0:T(4,128)(2,1)S(1)} %copy-done, s32[]{:T(128)S(6)} %select_n.109), kind=kLoop, calls=%fused_computation.46 | loop fusion | bytes 1048580 | tf_op jit(solution)/shard_map/jit(dynamic_index_in_dim)/dynamic_slice | solution.py:53
  42.4 1.0 convolution_convert_fusion.1.refs_4_
  43.4 0.1 copy.15
  43.6 1.4 %copy.16 = bf16[5,16,64,128]{3,2,1,0:T(8,128)(2,1)S(1)} copy(bf16[5,16,64,128]{3,2,0,1:T(8,128)(2,1)} %bitcast.8) | data formatting | bytes 2621440 | tf_op jit(solution)/shard_map/transpose | solution.py:89
  45.0 33.3 %shard_map.91 = bf16[768,256]{1,0:T(8,128)(2,1)S(1)} custom-call(s32[10]{0:T(128)S(1)} %pad_add_fusion.bounds_ref, bf16[4,768,128]{2,1,0:T(8,128)(2,1)S(1)} %pad_bitcast_fusion.q_ref, bf16[5,1024,128]{2,1,0:T(8,128)(2,1)S(1)} %bitcast.29, s32[5,1,1024]{2,1,0:T(1,128)S(1)} %get-tuple-element.12.refs_1_, bf16[5,1024,128]{2,1,0:T(8,128)(2,1)S(1)} %bitcast.30, ...), custom_call_target="tpu_custom_call" | custom-call | tf_op jit(solution)/shard_map/pallas_call | solution.py:205
  78.4 1.4 %collective-permute-done.1 = bf16[384,256]{1,0:T(8,128)(2,1)S(1)} collective-permute-done((bf16[384,256]{1,0:T(8,128)(2,1)S(1)}, bf16[384,256]{1,0:T(8,128)(2,1)S(1)}, u32[]{:S(2)}, u32[]{:S(2)}) %collective-permute-start.1) | collective-permute-done | bytes 196640 | tf_op jit(solution)/shard_map/ppermute | solution.py:107
  80.0 1.3 %broadcast_in_dim.21 = bf16[4,384,512]{2,1,0:T(8,128)(2,1)} broadcast(bf16[384,512]{1,0:T(8,128)(2,1)S(1)} %maximum_select_fusion), dimensions={1,2} | broadcast | bytes 1966080 | tf_op jit(solution)/shard_map/broadcast_in_dim | solution.py:113
  81.2 5.0 %all-to-all-start.1 = ((bf16[4,384,512]{2,1,0:T(8,128)(2,1)}), bf16[4,384,512]{2,1,0:T(8,128)(2,1)}, u32[]{:S(2)}, u32[]{:S(2)}) async-start(bf16[4,384,512]{2,1,0:T(8,128)(2,1)} %broadcast_in_dim.21), calls=%async_computation.1 | async-start | bytes 3145728 | tf_op jit(solution)/shard_map/all_to_all | solution.py:114
  86.3 3.1 %constant_dynamic-slice_fusion.2 = bf16[2048,512]{1,0:T(8,128)(2,1)} fusion(bf16[2048,2048]{1,0:T(8,128)(2,1)} %param.13, s32[]{:T(128)S(6)} %select_n.124), kind=kLoop, calls=%fused_computation.43 | loop fusion | bytes 4194308 | tf_op jit(solution)/shard_map/dynamic_slice | solution.py:116
  89.3 17.4 %all-to-all-done.1 = bf16[4,384,512]{2,1,0:T(8,128)(2,1)} async-done(((bf16[4,384,512]{2,1,0:T(8,128)(2,1)}), bf16[4,384,512]{2,1,0:T(8,128)(2,1)}, u32[]{:S(2)}, u32[]{:S(2)}) %all-to-all-start.1) | async-done | bytes 1572896 | tf_op jit(solution)/shard_map/all_to_all | solution.py:114
  106.8 3.0 %fusion.3 = bf16[384,512]{1,0:T(8,128)(2,1)S(1)} fusion(bf16[4,384,512]{2,1,0:T(8,128)(2,1)} %all-to-all-done.1, bf16[4,512,512]{2,1,0:T(8,128)(2,1)} %bitcast.33), kind=kOutput, calls=%fused_computation.9 | convolution fusion | flops 805502976 | bytes 4063232 | tf_op jit(solution)/shard_map/zrj,zjn->rn/dot_general | solution.py:118
  109.9 1.4 %collective-permute-start.2 = (bf16[384,256]{1,0:T(8,128)(2,1)S(1)}, bf16[384,256]{1,0:T(8,128)(2,1)S(1)}, u32[]{:S(2)}, u32[]{:S(2)}) collective-permute-start(bf16[384,256]{1,0:T(8,128)(2,1)S(1)} %get-tuple-element.8), channel_id=1, source_target_pairs={{0,1},{1,0},{2,3},{3,2},{4,5},{5,4},{6,7},{7,6},{8,9},{9,8},{10,11... | collective-permute-start | bytes 589832 | tf_op jit(solution)/shard_map/ppermute | solution.py:124
  111.3 1.1 collective-permute-done.2
  112.3 0.9 maximum_select_fusion.1
  (36 shorter events, 1.2 us)
Async XLA Ops:
  0.0 41.2 %copy-start = (bf16[2048,4,128]{2,1,0:T(4,128)(2,1)S(1)}, bf16[2048,4,128]{2,1,0:T(4,128)(2,1)}, u32[]{:S(2)}) copy-start(bf16[2048,4,128]{2,1,0:T(4,128)(2,1)} %param.12) | copy-start | bytes 6291460
  5.8 9.6 %copy-start.3 = (s32[80]{0:T(128)S(1)}, s32[80]{0:T(128)}, u32[]{:S(2)}) copy-start(s32[80]{0:T(128)} %param.17) | copy-start | bytes 964
  7.7 11.7 %copy-start.5 = (f32[2048]{0:T(1024)S(1)}, f32[2048]{0:T(1024)}, u32[]{:S(2)}) copy-start(f32[2048]{0:T(1024)} %param.10) | copy-start | bytes 24580
  7.7 26.0 %all-to-all-start = ((bf16[16,5,64,128]{3,2,1,0:T(8,128)(2,1)}), bf16[16,5,64,128]{3,2,1,0:T(8,128)(2,1)S(1)}, u32[]{:S(2)}, u32[]{:S(2)}) async-start(bf16[16,5,64,128]{3,2,1,0:T(8,128)(2,1)} %bitcast.32), calls=%async_computation | async-start | bytes 2621440 | tf_op jit(solution)/shard_map/all_to_all | solution.py:72
  16.6 2.8 %copy-start.1 = (bf16[768,2048]{1,0:T(8,128)(2,1)S(1)}, bf16[768,2048]{1,0:T(8,128)(2,1)}, u32[]{:S(2)}) copy-start(bf16[768,2048]{1,0:T(8,128)(2,1)} %param.9) | copy-start | bytes 9437188
  19.5 17.7 %copy-start.4 = (s32[80]{0:T(128)S(1)}, s32[80]{0:T(128)}, u32[]{:S(2)}) copy-start(s32[80]{0:T(128)} %param.16) | copy-start | bytes 964
  33.6 9.9 %collective-permute-start = (bf16[16,5,64,128]{3,2,1,0:T(8,128)(2,1)S(1)}, bf16[16,5,64,128]{3,2,1,0:T(8,128)(2,1)}, u32[]{:S(2)}, u32[]{:S(2)}) collective-permute-start(bf16[16,5,64,128]{3,2,1,0:T(8,128)(2,1)S(1)} %all-to-all-done), channel_id=1, source_target_pairs={{0,1},{1,0},{2,3},{3,2},{4,5},{5,4},{6,7},{7,6},{8,9},{9,8},{10,11... | collective-permute-start | bytes 3932168 | tf_op jit(solution)/shard_map/ppermute | solution.py:74
  39.6 2.8 %copy-start.2 = (bf16[768,2048]{1,0:T(8,128)(2,1)S(1)}, bf16[768,2048]{1,0:T(8,128)(2,1)}, u32[]{:S(2)}) copy-start(bf16[768,2048]{1,0:T(8,128)(2,1)} %param.9) | copy-start | bytes 9437188
  78.3 1.5 %collective-permute-start.1 = (bf16[384,256]{1,0:T(8,128)(2,1)S(1)}, bf16[384,256]{1,0:T(8,128)(2,1)S(1)}, u32[]{:S(2)}, u32[]{:S(2)}) collective-permute-start(bf16[384,256]{1,0:T(8,128)(2,1)S(1)} %get-tuple-element.10), channel_id=1, source_target_pairs={{0,1},{1,0},{2,3},{3,2},{4,5},{5,4},{6,7},{7,6},{8,9},{9,8},{10,11... | collective-permute-start | bytes 589832 | tf_op jit(solution)/shard_map/ppermute | solution.py:107
  81.2 25.6 %all-to-all-start.1 = ((bf16[4,384,512]{2,1,0:T(8,128)(2,1)}), bf16[4,384,512]{2,1,0:T(8,128)(2,1)}, u32[]{:S(2)}, u32[]{:S(2)}) async-start(bf16[4,384,512]{2,1,0:T(8,128)(2,1)} %broadcast_in_dim.21), calls=%async_computation.1 | async-start | bytes 3145728 | tf_op jit(solution)/shard_map/all_to_all | solution.py:114
  109.9 2.5 %collective-permute-start.2 = (bf16[384,256]{1,0:T(8,128)(2,1)S(1)}, bf16[384,256]{1,0:T(8,128)(2,1)S(1)}, u32[]{:S(2)}, u32[]{:S(2)}) collective-permute-start(bf16[384,256]{1,0:T(8,128)(2,1)S(1)} %get-tuple-element.8), channel_id=1, source_target_pairs={{0,1},{1,0},{2,3},{3,2},{4,5},{5,4},{6,7},{7,6},{8,9},{9,8},{10,11... | collective-permute-start | bytes 589832 | tf_op jit(solution)/shard_map/ppermute | solution.py:124

commit v9 on v7

--- a/solution.py
+++ b/solution.py
@@ -66,11 +66,15 @@
     held_slot = jnp.sum(jnp.where(holder == seq_index, local_slot, 0), axis=1)
     all_groups = request_groups.reshape(seq_count, DEVICE_REQUESTS)
     page_part = cache_pages.shape[2] // lax.axis_size("tc")
-    outgoing = lax.dynamic_slice_in_dim(
-        cache_pages[held_slot[all_groups], key_value_head], core_index * page_part, page_part, 2
-    )
+    head_pages = lax.dynamic_slice(
+        cache_pages,
+        (0, key_value_head, core_index * page_part, 0),
+        (cache_pages.shape[0], 1, page_part, cache_pages.shape[3]),
+    )[:, 0]
+    outgoing = head_pages[held_slot[all_groups]]
     incoming = lax.all_to_all(outgoing, "seq", 0, 0, tiled=True)
     core_count = lax.axis_size("tc")
+    incoming = incoming.transpose(1, 0, 2, 3)
     partner = lax.ppermute(incoming, "tc", [(0, 1), (1, 0)])
     source_ids = lax.iota(jnp.int32, seq_count)
     page_order = jnp.sum(
@@ -86,7 +90,7 @@
     key_parts = []
     for part, half in ((incoming, core_index), (partner, (core_index + 1) % core_count)):
         positions = (page_start + half * page_part + within).reshape(DEVICE_REQUESTS, 1, -1)
-        keys = part.transpose(1, 0, 2, 3).reshape(DEVICE_REQUESTS, -1, 2 * HEAD_SIZE)
+        keys = part.reshape(DEVICE_REQUESTS, -1, 2 * HEAD_SIZE)
         key_parts.append((keys, positions))
     starts = jnp.cumsum(lengths) - lengths
     bounds = jnp.concatenate([starts, starts + lengths]).astype(jnp.int32)

time: 119 us -> 114 us (0.958)
  local copies, waits for them, and re-layouts: 22.8 us -> 17.2 us
    gather x3, local copies, waits for them, and re-layouts: 7.61 us -> 3.17 us  [layer(): outgoing = head_pages[held_slot[all_groups]]]
    dynamic_slice x1 -> x0, local copies, waits for them, and re-layouts: 2.49 us -> none  [layer(): lax.dynamic_slice_in_dim(cache_pages[held_slot[all_groups], key_value_hea...]
    ppermute x0 -> x1, local copies, waits for them, and re-layouts: none -> 1.43 us  [layer(): partner = lax.ppermute(incoming, 'tc', [(0, 1), (1, 0)])]
    transpose x2 -> x1, local copies, waits for them, and re-layouts: 1.54 us -> 0.11 us  [layer(): incoming = incoming.transpose(1, 0, 2, 3)]
    squeeze x0 -> x1, local copies, waits for them, and re-layouts: none -> 1.31 us  [layer(): lax.dynamic_slice(cache_pages, (0, key_value_head, core_index * page_part...]
  transfers between devices with their start and end apart: 5 -> 5, of which waited for: 4 -> 4; matrix products, arithmetic and copies ran while one was open for 14% -> 15% of each run, Pallas kernels for 0% -> 0%
where the time goes in v9:
time: 114 us; the launch traced here: 113 us
  Pallas kernels  33.3 us (29%)
  waiting for transfers between devices  31.1 us (27%)
  starting transfers between devices  17.7 us (16%)
  local copies, waits for them, and re-layouts  17.2 us (15%)
  matrix products  7.42 us (7%)
  other arithmetic  6.13 us (5%)
    pallas_call x1, Pallas kernels, attend(): pl.pallas_call(functools.partial(attend_kernel, window), out_shape=jax.Sh...  33.3 us
    all_to_all x1, waiting for transfers between devices, layer(): chips_heads = lax.all_to_all(sent, 'tz', 0, 0, tiled=True)  17.5 us
    all_to_all x1, waiting for transfers between devices, layer(): incoming = lax.all_to_all(outgoing, 'seq', 0, 0, tiled=True)  10.8 us
    all_to_all x1, starting transfers between devices, layer(): incoming = lax.all_to_all(outgoing, 'seq', 0, 0, tiled=True)  7.7 us
    all_to_all x1, starting transfers between devices, layer(): chips_heads = lax.all_to_all(sent, 'tz', 0, 0, tiled=True)  5.02 us
    ppermute x1, starting transfers between devices, layer(): partner = lax.ppermute(incoming, 'tc', [(0, 1), (1, 0)])  3.49 us
    dot_general x1, matrix products, layer(): jnp.dot(normed, query_weight, preferred_element_type=jnp.float32)  3.33 us
    gather x3, local copies, waits for them, and re-layouts, layer(): outgoing = head_pages[held_slot[all_groups]]  3.17 us
  transfers between devices with their start and end apart: 5, of which 4 were waited for; matrix products, arithmetic and copies ran while one was open for 15% of the time, Pallas kernels for 0%

profile of v9, /device:TPU:1, one launch (start us, length us, event | category | flops | bytes accessed | tf_op | source)
XLA Modules:
  0.0 113.1 jit_solution(11500617348683920319)
XLA Ops:
  0.0 0.9 add_select_fusion.1
  0.9 0.7 reshape.176
  1.8 0.9 fusion.10
  2.7 1.2 %gather_fusion = s32[80]{0:T(128)S(1)} fusion(s32[16]{0:T(128)S(1)} %fusion.10, s32[1024]{0:T(1024)S(1)} %pad_clamp_fusion.2), kind=kCustom, calls=%fused_computation | custom fusion | bytes 960 | tf_op jit(solution)/shard_map/gather | solution.py:74
  4.0 0.1 reshape.190
  4.1 1.3 %dynamic-slice_bitcast_fusion = bf16[64,64,128]{2,1,0:T(8,128)(2,1)S(1)} fusion(bf16[64,4,128,128]{3,2,1,0:T(8,128)(2,1)} %param.14, s32[]{:T(128)S(6)} %select_n.97, s32[]{:T(128)S(6)} %select_n.98), kind=kLoop, calls=%fused_computation.12 | loop fusion | bytes 2097160 | tf_op jit(solution)/shard_map/squeeze | solution.py:69
  5.5 1.9 %gather_fusion.1 = bf16[80,64,128]{2,1,0:T(8,128)(2,1)} fusion(bf16[64,64,128]{2,1,0:T(8,128)(2,1)S(1)} %dynamic-slice_bitcast_fusion, s32[1024]{0:T(1024)S(1)} %pad_clamp_fusion.1), kind=kCustom, calls=%fused_computation.1 | custom fusion | bytes 2621760 | tf_op jit(solution)/shard_map/gather | solution.py:74
  7.3 7.7 %all-to-all-start = ((bf16[16,5,64,128]{3,2,1,0:T(8,128)(2,1)}), bf16[16,5,64,128]{3,2,1,0:T(8,128)(2,1)S(1)}, u32[]{:S(2)}, u32[]{:S(2)}) async-start(bf16[16,5,64,128]{3,2,1,0:T(8,128)(2,1)} %bitcast.32), calls=%async_computation | async-start | bytes 2621440 | tf_op jit(solution)/shard_map/all_to_all | solution.py:75
  15.1 0.1 select_reduce_fusion
  15.3 0.6 gather_fusion.2
  16.3 2.7 %fusion = f32[768]{0:T(1024)S(1)} fusion(bf16[768,2048]{1,0:T(8,128)(2,1)} %param.9), kind=kLoop, calls=%fused_computation.5 | loop fusion | flops 4717824 | bytes 3148800 | tf_op jit(solution)/shard_map/reduce_sum | solution.py:25
  19.1 3.3 %convolution_convert_fusion = bf16[768,256]{0,1:T(8,128)(2,1)} fusion(bf16[2048,256]{1,0:T(8,128)(2,1)} %param.11, bf16[768,2048]{1,0:T(8,128)(2,1)S(1)} %copy-done.1, f32[2048]{0:T(1024)S(1)} %copy-done.5, f32[768]{0:T(1024)S(1)} %add_rsqrt_fusion), kind=kOutput, calls=%fused_computation.10 | convolution fusion | flops 811794432 | bytes 4598784 | tf_op jit(solution)/shard_map/dot_general | solution.py:49
  22.4 10.8 %all-to-all-done = bf16[16,5,64,128]{3,2,1,0:T(8,128)(2,1)S(1)} async-done(((bf16[16,5,64,128]{3,2,1,0:T(8,128)(2,1)}), bf16[16,5,64,128]{3,2,1,0:T(8,128)(2,1)S(1)}, u32[]{:S(2)}, u32[]{:S(2)}) %all-to-all-start) | async-done | bytes 1310752 | tf_op jit(solution)/shard_map/all_to_all | solution.py:75
  33.3 3.5 %collective-permute-start = (bf16[5,16,64,128]{3,2,0,1:T(8,128)(2,1)S(1)}, bf16[5,16,64,128]{3,2,0,1:T(8,128)(2,1)}, u32[]{:S(2)}, u32[]{:S(2)}) collective-permute-start(bf16[5,16,64,128]{3,2,0,1:T(8,128)(2,1)S(1)} %bitcast.30), channel_id=1, source_target_pairs={{0,1},{1,0},{2,3},{3,2},{4,5},{5,4},{6,7},{7,6},{8,9},{9,8},{10,11... | collective-permute-start | bytes 3932168 | tf_op jit(solution)/shard_map/ppermute | solution.py:78
  36.9 0.2 reduce-window.9
  37.0 2.2 %copy.14 = bf16[768,4,64]{2,0,1:T(8,128)(2,1)} copy(bf16[768,4,64]{0,2,1:T(8,128)(2,1)} %bitcast.34) | data formatting | bytes 786432 | tf_op jit(solution)/shard_map/reshape | solution.py:52
  39.4 1.4 %pad_bitcast_fusion.q_ref = bf16[4,768,128]{2,1,0:T(8,128)(2,1)S(1)} fusion(bf16[768,4,64]{2,0,1:T(8,128)(2,1)} %copy.14), kind=kLoop, calls=%fused_computation.17 | loop fusion | bytes 1179648 | tf_op jit(solution)/shard_map/transpose | solution.py:100
  40.8 1.1 %constant_dynamic-slice_fusion.3 = bf16[2048,1,128]{2,1,0:T(2,128)(2,1)S(1)} fusion(bf16[2048,4,128]{2,1,0:T(4,128)(2,1)S(1)} %copy-done, s32[]{:T(128)S(6)} %select_n.97), kind=kLoop, calls=%fused_computation.50 | loop fusion | bytes 1048580 | tf_op jit(solution)/shard_map/jit(dynamic_index_in_dim)/dynamic_slice | solution.py:53
  42.0 1.0 convolution_convert_fusion.1.refs_4_
  43.1 0.1 copy.15
  43.2 1.4 %copy.16 = bf16[5,16,64,128]{3,2,1,0:T(8,128)(2,1)S(1)} copy(bf16[5,16,64,128]{3,2,0,1:T(8,128)(2,1)} %collective-permute-done) | data formatting | bytes 2621440 | tf_op jit(solution)/shard_map/ppermute | solution.py:78
  44.6 33.3 %shard_map.91 = bf16[768,256]{1,0:T(8,128)(2,1)S(1)} custom-call(s32[10]{0:T(128)S(1)} %pad_add_fusion.bounds_ref, bf16[4,768,128]{2,1,0:T(8,128)(2,1)S(1)} %pad_bitcast_fusion.q_ref, bf16[5,1024,128]{2,1,0:T(8,128)(2,1)S(1)} %bitcast.28, s32[5,1,1024]{2,1,0:T(1,128)S(1)} %get-tuple-element.10.refs_1_, bf16[5,1024,128]{2,1,0:T(8,128)(2,1)S(1)} %bitcast.29, ...), custom_call_target="tpu_custom_call" | custom-call | tf_op jit(solution)/shard_map/pallas_call | solution.py:206
  78.0 1.7 %collective-permute-done.1 = bf16[768,256]{1,0:T(8,128)(2,1)S(1)} collective-permute-done((bf16[768,256]{1,0:T(8,128)(2,1)S(1)}, bf16[768,256]{1,0:T(8,128)(2,1)S(1)}, u32[]{:S(2)}, u32[]{:S(2)}) %collective-permute-start.1) | collective-permute-done | bytes 393248 | tf_op jit(solution)/shard_map/ppermute | solution.py:105
  79.7 0.1 fusion.7
  79.8 1.3 %broadcast_in_dim.21 = bf16[4,384,512]{2,1,0:T(8,128)(2,1)} broadcast(bf16[384,512]{1,0:T(8,128)(2,1)S(1)} %fusion.7), dimensions={1,2} | broadcast | bytes 1966080 | tf_op jit(solution)/shard_map/broadcast_in_dim | solution.py:114
  81.1 5.0 %all-to-all-start.1 = ((bf16[4,384,512]{2,1,0:T(8,128)(2,1)}), bf16[4,384,512]{2,1,0:T(8,128)(2,1)}, u32[]{:S(2)}, u32[]{:S(2)}) async-start(bf16[4,384,512]{2,1,0:T(8,128)(2,1)} %broadcast_in_dim.21), calls=%async_computation.1 | async-start | bytes 3145728 | tf_op jit(solution)/shard_map/all_to_all | solution.py:115
  86.1 3.1 %constant_dynamic-slice_fusion.2 = bf16[2048,512]{1,0:T(8,128)(2,1)} fusion(bf16[2048,2048]{1,0:T(8,128)(2,1)} %param.13, s32[]{:T(128)S(6)} %select_n.109), kind=kLoop, calls=%fused_computation.49 | loop fusion | bytes 4194308 | tf_op jit(solution)/shard_map/dynamic_slice | solution.py:117
  89.2 17.5 %all-to-all-done.1 = bf16[4,384,512]{2,1,0:T(8,128)(2,1)} async-done(((bf16[4,384,512]{2,1,0:T(8,128)(2,1)}), bf16[4,384,512]{2,1,0:T(8,128)(2,1)}, u32[]{:S(2)}, u32[]{:S(2)}) %all-to-all-start.1) | async-done | bytes 1572896 | tf_op jit(solution)/shard_map/all_to_all | solution.py:115
  106.7 3.0 %fusion.3 = bf16[384,512]{1,0:T(8,128)(2,1)S(1)} fusion(bf16[4,384,512]{2,1,0:T(8,128)(2,1)} %all-to-all-done.1, bf16[4,512,512]{2,1,0:T(8,128)(2,1)} %bitcast.33), kind=kOutput, calls=%fused_computation.9 | convolution fusion | flops 805502976 | bytes 4063232 | tf_op jit(solution)/shard_map/zrj,zjn->rn/dot_general | solution.py:119
  109.7 1.4 %collective-permute-start.2 = (bf16[384,256]{1,0:T(8,128)(2,1)S(1)}, bf16[384,256]{1,0:T(8,128)(2,1)S(1)}, u32[]{:S(2)}, u32[]{:S(2)}) collective-permute-start(bf16[384,256]{1,0:T(8,128)(2,1)S(1)} %get-tuple-element.8), channel_id=1, source_target_pairs={{0,1},{1,0},{2,3},{3,2},{4,5},{5,4},{6,7},{7,6},{8,9},{9,8},{10,11... | collective-permute-start | bytes 589832 | tf_op jit(solution)/shard_map/ppermute | solution.py:125
  111.2 1.1 collective-permute-done.2
  112.2 0.9 maximum_select_fusion
  (35 shorter events, 1.2 us)
Async XLA Ops:
  0.0 40.8 %copy-start = (bf16[2048,4,128]{2,1,0:T(4,128)(2,1)S(1)}, bf16[2048,4,128]{2,1,0:T(4,128)(2,1)}, u32[]{:S(2)}) copy-start(bf16[2048,4,128]{2,1,0:T(4,128)(2,1)} %param.12) | copy-start | bytes 6291460
  5.4 9.6 %copy-start.3 = (s32[80]{0:T(128)S(1)}, s32[80]{0:T(128)}, u32[]{:S(2)}) copy-start(s32[80]{0:T(128)} %param.17) | copy-start | bytes 964
  7.3 11.7 %copy-start.5 = (f32[2048]{0:T(1024)S(1)}, f32[2048]{0:T(1024)}, u32[]{:S(2)}) copy-start(f32[2048]{0:T(1024)} %param.10) | copy-start | bytes 24580
  7.3 26.0 %all-to-all-start = ((bf16[16,5,64,128]{3,2,1,0:T(8,128)(2,1)}), bf16[16,5,64,128]{3,2,1,0:T(8,128)(2,1)S(1)}, u32[]{:S(2)}, u32[]{:S(2)}) async-start(bf16[16,5,64,128]{3,2,1,0:T(8,128)(2,1)} %bitcast.32), calls=%async_computation | async-start | bytes 2621440 | tf_op jit(solution)/shard_map/all_to_all | solution.py:75
  16.3 2.8 %copy-start.1 = (bf16[768,2048]{1,0:T(8,128)(2,1)S(1)}, bf16[768,2048]{1,0:T(8,128)(2,1)}, u32[]{:S(2)}) copy-start(bf16[768,2048]{1,0:T(8,128)(2,1)} %param.9) | copy-start | bytes 9437188
  19.1 17.7 %copy-start.4 = (s32[80]{0:T(128)S(1)}, s32[80]{0:T(128)}, u32[]{:S(2)}) copy-start(s32[80]{0:T(128)} %param.16) | copy-start | bytes 964
  33.3 9.9 %collective-permute-start = (bf16[5,16,64,128]{3,2,0,1:T(8,128)(2,1)S(1)}, bf16[5,16,64,128]{3,2,0,1:T(8,128)(2,1)}, u32[]{:S(2)}, u32[]{:S(2)}) collective-permute-start(bf16[5,16,64,128]{3,2,0,1:T(8,128)(2,1)S(1)} %bitcast.30), channel_id=1, source_target_pairs={{0,1},{1,0},{2,3},{3,2},{4,5},{5,4},{6,7},{7,6},{8,9},{9,8},{10,11... | collective-permute-start | bytes 3932168 | tf_op jit(solution)/shard_map/ppermute | solution.py:78
  39.2 2.8 %copy-start.2 = (bf16[768,2048]{1,0:T(8,128)(2,1)S(1)}, bf16[768,2048]{1,0:T(8,128)(2,1)}, u32[]{:S(2)}) copy-start(bf16[768,2048]{1,0:T(8,128)(2,1)} %param.9) | copy-start | bytes 9437188
  77.9 1.8 %collective-permute-start.1 = (bf16[768,256]{1,0:T(8,128)(2,1)S(1)}, bf16[768,256]{1,0:T(8,128)(2,1)S(1)}, u32[]{:S(2)}, u32[]{:S(2)}) collective-permute-start(bf16[768,256]{1,0:T(8,128)(2,1)S(1)} %shard_map.91), channel_id=1, source_target_pairs={{0,1},{1,0},{2,3},{3,2},{4,5},{5,4},{6,7},{7,6},{8,9},{9,8},{10,11... | collective-permute-start | bytes 1179656 | tf_op jit(solution)/shard_map/ppermute | solution.py:105
  81.1 25.6 %all-to-all-start.1 = ((bf16[4,384,512]{2,1,0:T(8,128)(2,1)}), bf16[4,384,512]{2,1,0:T(8,128)(2,1)}, u32[]{:S(2)}, u32[]{:S(2)}) async-start(bf16[4,384,512]{2,1,0:T(8,128)(2,1)} %broadcast_in_dim.21), calls=%async_computation.1 | async-start | bytes 3145728 | tf_op jit(solution)/shard_map/all_to_all | solution.py:115
  109.7 2.5 %collective-permute-start.2 = (bf16[384,256]{1,0:T(8,128)(2,1)S(1)}, bf16[384,256]{1,0:T(8,128)(2,1)S(1)}, u32[]{:S(2)}, u32[]{:S(2)}) collective-permute-start(bf16[384,256]{1,0:T(8,128)(2,1)S(1)} %get-tuple-element.8), channel_id=1, source_target_pairs={{0,1},{1,0},{2,3},{3,2},{4,5},{5,4},{6,7},{7,6},{8,9},{9,8},{10,11... | collective-permute-start | bytes 589832 | tf_op jit(solution)/shard_map/ppermute | solution.py:125
